TPU v7x, 128 devices: a whole 4x4x4 slice. The times are simulated.
128 devices in a mesh: head: 2 (over core), req: 64 (over x, y, z).
Axes of the slice: x: 4, y: 4, z: 4, core: 2. Of those that a mesh axis runs over, the one named last changes fastest.
Arguments:
- queries: bfloat16 [512, 8192], P('req', 'head'), may hold values from -9 to 9
- new_key: bfloat16 [512, 1024], P('req', 'head'), may hold values from -4 to 4
- new_value: bfloat16 [512, 1024], P('req', 'head'), may hold values from -4 to 4
- key_cache: bfloat16 [5888, 64, 1024], P('req', None, 'head'), may hold values from -4 to 4
- value_cache: bfloat16 [5888, 64, 1024], P('req', None, 'head'), may hold values from -4 to 4
- lengths: int32 [512], P('req'), may hold values from 1 to 4096, as said below
- page_table: int32 [512, 64], P('req'), may hold values from 0 to 91, as said below
- residual: bfloat16 [512, 8192], P(None, ('head', 'req')), may hold values from -6 to 6
- out_weight: bfloat16 [8192, 8192], P(None, ('head', 'req')), may hold values from -0.25 to 0.25
- gate_weight: bfloat16 [8192, 28672], P('head', 'req'), may hold values from -0.0625 to 0.0625
- up_weight: bfloat16 [8192, 28672], P('head', 'req'), may hold values from -0.0625 to 0.0625
- down_weight: bfloat16 [28672, 8192], P('req', 'head'), may hold values from -0.09375 to 0.09375
Outputs:
- layer_out: bfloat16 [512, 8192], P(None, ('head', 'req'))
Inputs may be any that keep to these rules, and one draw needn't show every extreme that they name: `lengths`: the 8 requests of one index of req hold at most one request of length 4096 and all others at most 256; each such group holds one request of length exactly 256, and some group holds one of length 4096. `page_table`: for request r the first ceil(lengths[r] / 64) entries name distinct pages of the pool of index r // 8 of req, and no page serves two requests; the other entries are arbitrary offsets and are not read.
All inputs are finite; a program needn't handle non-finite values.
Results may differ from a plain program's by a relative error of at most 0.01.
Values may be sent and summed in bfloat16 or wider, within the bound.
No kernel may reach another device: no remote copies, remote signals or barrier semaphores. Data moves between devices by JAX's collectives and lax.ppermute only.
A program may use at most 192 MiB of HBM per device.

v0:
```python
import jax
import jax.numpy as jnp
from jax import lax
from jax.sharding import PartitionSpec as P

HD = 128


def attend_padded(queries, new_key, new_value, key_pool, value_pool, lengths, page_table):
    row_count = queries.shape[0]
    kv_width = key_pool.shape[2]
    groups = kv_width // HD
    per_group = queries.shape[1] // kv_width
    key_span = page_table.shape[1] * key_pool.shape[1]
    key_rows = key_pool[page_table].reshape(row_count, key_span, groups, HD)
    value_rows = value_pool[page_table].reshape(row_count, key_span, groups, HD)
    grouped = queries.reshape(row_count, groups, per_group, HD)
    scores = jnp.einsum(
        "rgqd,rtgd->rgqt", grouped, key_rows, preferred_element_type=jnp.float32
    ) * HD ** (-0.5)
    own_score = jnp.einsum(
        "rgqd,rgd->rgq",
        grouped,
        new_key.reshape(row_count, groups, HD),
        preferred_element_type=jnp.float32,
    ) * HD ** (-0.5)
    live_mask = (lax.broadcasted_iota(jnp.int32, (row_count, key_span), 1) < lengths[:, None])[
        :, None, None, :
    ]
    top_score = jnp.maximum(jnp.max(jnp.where(live_mask, scores, -1e30), axis=3), own_score)
    exp_terms = jnp.where(live_mask, jnp.exp(scores - top_score[..., None]), 0.0)
    own_exp = jnp.exp(own_score - top_score)
    total_mass = jnp.sum(exp_terms, axis=3) + own_exp
    weights = (exp_terms / total_mass[..., None]).astype(jnp.bfloat16)
    own_weight = (own_exp / total_mass).astype(jnp.bfloat16)
    summed = jnp.einsum("rgqt,rtgd->rgqd", weights, value_rows, preferred_element_type=jnp.float32)
    summed = summed + own_weight.astype(jnp.float32)[..., None] * new_value.reshape(
        row_count, groups, 1, HD
    ).astype(jnp.float32)
    return summed.reshape(row_count, -1).astype(jnp.bfloat16)


def body(
    queries,
    new_key,
    new_value,
    key_cache,
    value_cache,
    lengths,
    page_table,
    residual,
    out_weight,
    gate_weight,
    up_weight,
    down_weight,
):
    attention = attend_padded(
        queries, new_key, new_value, key_cache, value_cache, lengths, page_table
    )
    features = lax.all_gather(attention, "head", axis=1, tiled=True)
    attn_update = jnp.dot(
        lax.all_gather(features, "req", axis=0, tiled=True),
        out_weight,
        preferred_element_type=jnp.float32,
    )
    mixed_rows = (residual.astype(jnp.float32) + attn_update).astype(jnp.bfloat16)
    shard_piece = lax.all_gather(mixed_rows, "req", axis=1, tiled=True)
    gate_acts = jnp.dot(shard_piece, gate_weight, preferred_element_type=jnp.float32)
    up_acts = jnp.dot(shard_piece, up_weight, preferred_element_type=jnp.float32)
    gate_full, up_full = lax.psum((gate_acts, up_acts), "head")
    hidden = (jax.nn.silu(gate_full) * up_full).astype(jnp.bfloat16)
    down_part = lax.psum_scatter(
        lax.dot_general(
            down_weight, hidden, (((0,), (1,)), ((), ())), preferred_element_type=jnp.float32
        ),
        "req",
        scatter_dimension=0,
        tiled=True,
    )
    return (mixed_rows.astype(jnp.float32) + down_part.T).astype(jnp.bfloat16)


def solution(mesh):
    return jax.shard_map(
        body,
        mesh=mesh,
        in_specs=(
            P("req", "head"),
            P("req", "head"),
            P("req", "head"),
            P("req", None, "head"),
            P("req", None, "head"),
            P("req"),
            P("req", None),
            P(None, ("head", "req")),
            P(None, ("head", "req")),
            P("head", "req"),
            P("head", "req"),
            P("req", "head"),
        ),
        out_specs=P(None, ("head", "req")),
        check_vma=False,
    )
```

profile of v0, /device:TPU:0, one launch (start us, length us, event | category | flops | bytes accessed | tf_op | source)
XLA Modules:
  0.0 760.0 jit_solution(4874620269207876613)
XLA Ops:
  6.5 0.8 iota_compare_fusion
  7.4 0.7 compare_select_fusion
  8.1 0.1 reshape.49
  8.2 18.8 %gather_fusion = bf16[512,64,512]{2,1,0:T(8,128)(2,1)} fusion(bf16[92,64,512]{2,1,0:T(8,128)(2,1)} %param.15, s32[1024]{0:T(1024)S(1)} %pad_clamp_fusion), kind=kCustom, calls=%fused_computation | custom fusion | bytes 67110912 | tf_op jit(solution)/shard_map/gather | solution.py:15
  27.0 46.2 %reshape.42 = bf16[8,4096,4,128]{3,2,1,0:T(4,128)(2,1)} reshape(bf16[512,64,512]{2,1,0:T(8,128)(2,1)} %gather_fusion) | data formatting | bytes 67108864 | tf_op jit(solution)/shard_map/reshape | solution.py:15
  73.2 0.2 fusion.31
  73.4 18.8 %select_reduce_fusion = (f32[8,4,8]{2,1,0:T(4,128)S(1)}, f32[8,4,4096,8]{2,3,1,0:T(8,128)S(1)}) fusion(pred[8,4096]{1,0:T(8,128)(4,1)S(1)} %iota_compare_fusion, bf16[8,4,8,128]{3,0,2,1:T(8,128)(2,1)S(1)} %bitcast.44, bf16[8,4096,4,128]{3,2,1,0:T(4,128)(2,1)} %reshape.42), kind=kOutput, calls=%fused_computation.12 | convolution fusion | flops 271580928 | bytes 37848064 | tf_op jit(solution)/shard_map/rgqd,rtgd->rgqt/dot_general | solution.py:18
  92.2 2.0 copy-done.1
  94.2 1.1 bitcast_reduce_fusion
  95.3 19.0 %gather_fusion.1 = bf16[512,64,512]{2,1,0:T(8,128)(2,1)} fusion(bf16[92,64,512]{2,1,0:T(8,128)(2,1)} %param.16, s32[1024]{0:T(1024)S(1)} %pad_clamp_fusion), kind=kCustom, calls=%fused_computation.1 | custom fusion | bytes 67110912 | tf_op jit(solution)/shard_map/gather | solution.py:16
  114.3 46.0 %reshape.45 = bf16[8,4096,4,128]{3,2,1,0:T(4,128)(2,1)} reshape(bf16[512,64,512]{2,1,0:T(8,128)(2,1)} %gather_fusion.1) | data formatting | bytes 67108864 | tf_op jit(solution)/shard_map/reshape | solution.py:16
  160.3 19.9 %fusion.24 = bf16[1,8,32,128]{3,2,1,0:T(8,128)(2,1)S(1)} fusion(bf16[8,4096,4,128]{3,2,1,0:T(4,128)(2,1)} %reshape.45, f32[8,4,4096,8]{2,3,1,0:T(8,128)} %copy-done.1, f32[8,4,8]{2,1,0:T(4,128)S(1)} %get-tuple-element.8, f32[8,4,8]{2,1,0:T(4,128)S(1)} %multiply_maximum_fusion, pred[8,4096]{1,0:T(8,128)(4,1)S(1)} %iota_compare_fusion, ...), kind=kOutput, calls=%fused_computation.21 | convolution fusion | flops 272728064 | bytes 37866496 | tf_op jit(solution)/shard_map/rgqt,rtgd->rgqd/dot_general | solution.py:36
  180.2 2.0 all_gather.9
  182.3 81.0 %all-gather.3.cloned.1.call-done = bf16[512,8192]{1,0:T(8,128)(2,1)} async-done(((bf16[8,8192]{1,0:T(8,128)(2,1)}), bf16[512,8192]{1,0:T(8,128)(2,1)}) %all-gather.3.cloned.1.call-update) | async-done | bytes 8388624 | tf_op jit(solution)/shard_map/all_gather | solution.py:62
  263.3 6.7 fusion.23
  270.0 0.0 all-reduce.3.cloned.1.call-start
  270.0 68.2 %all-gather.5.cloned.1.call-done = bf16[512,4096]{0,1:T(8,128)(2,1)} async-done(((bf16[512,64]{0,1:T(8,128)(2,1)}), bf16[512,4096]{0,1:T(8,128)(2,1)}) %all-gather.5.cloned.1.call-update) | async-done | bytes 4194320 | tf_op jit(solution)/shard_map/all_gather | solution.py:67
  338.3 6.4 fusion.39
  344.7 3.0 fusion.40
  347.8 0.3 reduce-scatter.2.cloned.1.call-start
  348.0 23.7 %all-reduce.3.cloned.1.call-done = (f32[512,448]{0,1:T(8,128)}, f32[512,448]{0,1:T(8,128)}) async-done(((f32[512,448]{0,1:T(8,128)}, f32[512,448]{0,1:T(8,128)}), (f32[512,448]{0,1:T(8,128)}, f32[512,448]{0,1:T(8,128)})) %all-reduce.3.cloned.1.call-update) | async-done | bytes 1835024 | tf_op jit(solution)/shard_map/psum | solution.py:70
  371.8 8.3 %convolution_bitcast_fusion = f32[4096,512]{1,0:T(8,128)} fusion(bf16[448,4096]{1,0:T(8,128)(2,1)} %param.23, f32[512,448]{0,1:T(8,128)} %get-tuple-element.5, f32[512,448]{0,1:T(8,128)} %get-tuple-element.6), kind=kOutput, calls=%fused_computation.6 | convolution fusion | flops 1880424448 | bytes 13893632 | tf_op jit(solution)/shard_map/dot_general | solution.py:73
  380.1 371.8 %reduce-scatter.2.cloned.1.call-done = f32[64,512]{1,0:T(8,128)} async-done(((f32[4096,512]{1,0:T(8,128)}), f32[64,512]{1,0:T(8,128)}) %reduce-scatter.2.cloned.1.call-update) | async-done | bytes 131088 | tf_op jit(solution)/shard_map/reduce_scatter | solution.py:72
  751.9 1.5 fusion.30
  (29 shorter events, 0.2 us)
Async XLA Ops:
  6.5 256.8 %copy-start = (bf16[8192,64]{0,1:T(8,128)(2,1)S(1)}, bf16[8192,64]{0,1:T(8,128)(2,1)}, u32[]{:S(2)}) copy-start(bf16[8192,64]{0,1:T(8,128)(2,1)} %param.20) | copy-start | bytes 3145732
  6.5 256.8 %all-gather.3.cloned.1.call-start = ((), (), s32[]{:S(2)}) async-start(), calls=%async_computation.1 | async-start | bytes 8519680 | tf_op jit(solution)/shard_map/all_gather | solution.py:62
  27.0 46.2 %copy-start.7 = (bf16[8,4096]{1,0:T(8,128)(2,1)S(1)}, bf16[8,4096]{1,0:T(8,128)(2,1)}, u32[]{:S(2)}) copy-start(bf16[8,4096]{1,0:T(8,128)(2,1)} %param.12) | copy-start | bytes 196612
  27.0 46.2 %copy-start.8 = (bf16[8,512]{1,0:T(8,128)(2,1)S(1)}, bf16[8,512]{1,0:T(8,128)(2,1)}, u32[]{:S(2)}) copy-start(bf16[8,512]{1,0:T(8,128)(2,1)} %param.13) | copy-start | bytes 24580
  92.2 2.0 copy-start.1
  114.3 46.0 %copy-start.4 = (bf16[8,512]{1,0:T(8,128)(2,1)S(1)}, bf16[8,512]{1,0:T(8,128)(2,1)}, u32[]{:S(2)}) copy-start(bf16[8,512]{1,0:T(8,128)(2,1)} %param.14) | copy-start | bytes 24580
  160.2 103.0 %copy-start.3 = (bf16[512,64]{0,1:T(8,128)(2,1)S(1)}, bf16[512,64]{0,1:T(8,128)(2,1)}, u32[]{:S(2)}) copy-start(bf16[512,64]{0,1:T(8,128)(2,1)} %param.19) | copy-start | bytes 196612
  182.3 156.0 %all-gather.5.cloned.1.call-start = ((), (), s32[]{:S(2)}) async-start(), calls=%async_computation.2 | async-start | bytes 4259840 | tf_op jit(solution)/shard_map/all_gather | solution.py:67
  270.0 101.8 %all-reduce.3.cloned.1.call-start = ((), (), s32[]{:S(2)}) async-start(), calls=%async_computation.4 | async-start | bytes 3670016 | tf_op jit(solution)/shard_map/psum | solution.py:70
  338.3 6.4 copy-start.5
  338.3 6.4 copy-start.6
  347.8 404.1 %reduce-scatter.2.cloned.1.call-start = ((), (), s32[]{:S(2)}) async-start(), calls=%async_computation.3 | async-start | bytes 8519680 | tf_op jit(solution)/shard_map/reduce_scatter | solution.py:72
  380.1 371.8 %copy-start.2 = (bf16[512,64]{0,1:T(8,128)(2,1)S(1)}, bf16[512,64]{0,1:T(8,128)(2,1)}, u32[]{:S(2)}) copy-start(bf16[512,64]{0,1:T(8,128)(2,1)} %fusion.23) | copy-start | bytes 196612
Sparse Core Ops, SparseCore 0:
  182.4 80.8 all-gather.2
  270.1 68.1 all-gather.4
  347.9 23.8 all-reduce.2
  380.2 371.6 reduce-scatter.1
where the time goes:
time: 763 us; the launch traced here: 760 us
  waiting for transfers between devices  545 us (71%)
  local copies, waits for them, and re-layouts  132 us (17%)
  matrix products  63.3 us (8%)
  between operations  13.2 us (2%)
    reduce_scatter x1, waiting for transfers between devices, body(): lax.psum_scatter(lax.dot_general(down_weight, hidden, (((0,), (1,)), ((),...  372 us
    all_gather x1, waiting for transfers between devices, body(): lax.all_gather(features, 'req', axis=0, tiled=True)  81 us
    all_gather x1, waiting for transfers between devices, body(): shard_piece = lax.all_gather(mixed_rows, 'req', axis=1, tiled=True)  68.2 us
    reshape x1, local copies, waits for them, and re-layouts, attend_padded(): key_rows = key_pool[page_table].reshape(row_count, key_span, groups, HD)  46.2 us
    reshape x1, local copies, waits for them, and re-layouts, attend_padded(): value_rows = value_pool[page_table].reshape(row_count, key_span, groups, HD)  46 us
    psum x1, waiting for transfers between devices, body(): gate_full, up_full = lax.psum((gate_acts, up_acts), 'head')  23.7 us
    dot_general x1, matrix products, attend_padded(): jnp.einsum('rgqt,rtgd->rgqd', weights, value_rows, preferred_element_type...  19.9 us
    gather x1, local copies, waits for them, and re-layouts, attend_padded(): value_rows = value_pool[page_table].reshape(row_count, key_span, groups, HD)  19 us
  transfers between devices with their start and end apart: 4, of which 4 were waited for; matrix products, arithmetic and copies ran while one was open for 0% of the time, Pallas kernels for 0%

commit v1 on v0

v1 whole, which is shorter than its diff:
```python
import jax
import jax.numpy as jnp
from jax import lax
from jax.sharding import PartitionSpec as P

HD = 128


def attend_pool(queries, new_key, new_value, key_pool, value_pool, lengths, page_table):
    row_count = queries.shape[0]
    pool_pages, page_rows, kv_width = key_pool.shape
    groups = kv_width // HD
    per_group = queries.shape[1] // kv_width
    pages_max = page_table.shape[1]
    pool_len = pool_pages * page_rows

    slot_start = lax.broadcasted_iota(jnp.int32, (row_count, pages_max), 1) * page_rows
    slot_live = slot_start < lengths[:, None]
    match = (page_table[:, :, None] == lax.broadcasted_iota(jnp.int32, (1, 1, pool_pages), 2)) & slot_live[
        :, :, None
    ]
    owned = jnp.any(match, axis=1)
    base = jnp.sum(jnp.where(match, slot_start[:, :, None], 0), axis=1)
    position = base[:, :, None] + lax.broadcasted_iota(jnp.int32, (1, 1, page_rows), 2)
    live_mask = (owned[:, :, None] & (position < lengths[:, None, None])).reshape(row_count, pool_len)
    live_mask = live_mask[:, None, None, :]

    key_rows = key_pool.reshape(pool_len, groups, HD)
    value_rows = value_pool.reshape(pool_len, groups, HD)
    grouped = queries.reshape(row_count, groups, per_group, HD)
    scores = jnp.einsum(
        "rgqd,tgd->rgqt", grouped, key_rows, preferred_element_type=jnp.float32
    ) * HD ** (-0.5)
    own_score = jnp.einsum(
        "rgqd,rgd->rgq",
        grouped,
        new_key.reshape(row_count, groups, HD),
        preferred_element_type=jnp.float32,
    ) * HD ** (-0.5)
    top_score = jnp.maximum(jnp.max(jnp.where(live_mask, scores, -1e30), axis=3), own_score)
    exp_terms = jnp.where(live_mask, jnp.exp(scores - top_score[..., None]), 0.0)
    own_exp = jnp.exp(own_score - top_score)
    total_mass = jnp.sum(exp_terms, axis=3) + own_exp
    weights = (exp_terms / total_mass[..., None]).astype(jnp.bfloat16)
    own_weight = (own_exp / total_mass).astype(jnp.bfloat16)
    summed = jnp.einsum("rgqt,tgd->rgqd", weights, value_rows, preferred_element_type=jnp.float32)
    summed = summed + own_weight.astype(jnp.float32)[..., None] * new_value.reshape(
        row_count, groups, 1, HD
    ).astype(jnp.float32)
    return summed.reshape(row_count, -1).astype(jnp.bfloat16)


def body(
    queries,
    new_key,
    new_value,
    key_cache,
    value_cache,
    lengths,
    page_table,
    residual,
    out_weight,
    gate_weight,
    up_weight,
    down_weight,
):
    n_req = lax.axis_size("req")
    head = lax.axis_index("head")
    swap = [(0, 1), (1, 0)]
    half = out_weight.shape[0] // 2
    cols = out_weight.shape[1]

    partner_rows = lax.dynamic_slice_in_dim(out_weight, (1 - head) * half, half, axis=0)
    lent_rows = lax.ppermute(partner_rows, "head", swap)
    own_rows = lax.dynamic_slice_in_dim(out_weight, head * half, half, axis=0)

    attention = attend_pool(
        queries, new_key, new_value, key_cache, value_cache, lengths, page_table
    )
    features = lax.all_gather(attention, "req", axis=0, tiled=True)
    both = jnp.dot(
        features,
        jnp.concatenate([own_rows, lent_rows], axis=1),
        preferred_element_type=jnp.float32,
    )
    attn_update = both[:, :cols] + lax.ppermute(both[:, cols:], "head", swap)
    mixed_rows = (residual.astype(jnp.float32) + attn_update).astype(jnp.bfloat16)
    shard_piece = lax.all_gather(mixed_rows, "req", axis=1, tiled=True)
    gate_acts = jnp.dot(shard_piece, gate_weight, preferred_element_type=jnp.float32)
    up_acts = jnp.dot(shard_piece, up_weight, preferred_element_type=jnp.float32)
    gate_full, up_full = lax.psum((gate_acts, up_acts), "head")
    hidden = (jax.nn.silu(gate_full) * up_full).astype(jnp.bfloat16)
    down_acts = jnp.dot(hidden, down_weight, preferred_element_type=jnp.float32)
    tokens = down_acts.shape[0]
    pieces = (
        down_acts.astype(jnp.bfloat16)
        .reshape(tokens, n_req, down_acts.shape[1] // n_req)
        .transpose(1, 0, 2)
    )
    gathered = lax.all_to_all(pieces, "req", 0, 0, tiled=True)
    down_part = jnp.sum(gathered.astype(jnp.float32), axis=0)
    return (mixed_rows.astype(jnp.float32) + down_part).astype(jnp.bfloat16)


def solution(mesh):
    return jax.shard_map(
        body,
        mesh=mesh,
        in_specs=(
            P("req", "head"),
            P("req", "head"),
            P("req", "head"),
            P("req", None, "head"),
            P("req", None, "head"),
            P("req"),
            P("req", None),
            P(None, ("head", "req")),
            P(None, ("head", "req")),
            P("head", "req"),
            P("head", "req"),
            P("req", "head"),
        ),
        out_specs=P(None, ("head", "req")),
        check_vma=False,
    )
```

time: 763 us -> 311 us (0.41)
  waiting for transfers between devices: 545 us -> 162 us
  local copies, waits for them, and re-layouts: 132 us -> 33 us
  blocking collectives: 2.03 us -> 63.1 us
  matrix products: 63.3 us -> 32.2 us
    reduce_scatter x1 -> x0, waiting for transfers between devices: 372 us -> none  [body(): lax.psum_scatter(lax.dot_general(down_weight, hidden, (((0,), (1,)), ((),...]
    reshape x2, local copies, waits for them, and re-layouts: 92.2 us -> 22.2 us  [the longest x1 11.1 us: attend_pool(): key_rows = key_pool.reshape(pool_len, groups, HD)]
    all_to_all x0 -> x1, blocking collectives: none -> 63.1 us  [body(): gathered = lax.all_to_all(pieces, 'req', 0, 0, tiled=True)]
    gather x2 -> x0, local copies, waits for them, and re-layouts: 37.8 us -> none  [the longest x1 19 us: attend_padded(): value_rows = value_pool[page_table].reshape(row_count, key_span, groups, HD)]
    dot_general x5, matrix products: 53.9 us -> 22.8 us  [the longest x1 6.99 us: body(): down_acts = jnp.dot(hidden, down_weight, preferred_element_type=jnp.float32)]
    all_gather x1, waiting for transfers between devices: 81 us -> 69.1 us  [body(): features = lax.all_gather(attention, 'req', axis=0, tiled=True)]
  transfers between devices with their start and end apart: 4 -> 5, of which waited for: 4 -> 5; matrix products, arithmetic and copies ran while one was open for 0% -> 0% of each run, Pallas kernels for 0% -> 0%
where the time goes in v1:
time: 311 us; the launch traced here: 310 us
  waiting for transfers between devices  162 us (52%)
  blocking collectives  63.1 us (20%)
  local copies, waits for them, and re-layouts  33 us (11%)
  matrix products  32.2 us (10%)
  between operations  13.3 us (4%)
  other arithmetic  6.13 us (2%)
    all_gather x1, waiting for transfers between devices, body(): features = lax.all_gather(attention, 'req', axis=0, tiled=True)  69.1 us
    all_gather x1, waiting for transfers between devices, body(): shard_piece = lax.all_gather(mixed_rows, 'req', axis=1, tiled=True)  65.9 us
    all_to_all x1, blocking collectives, body(): gathered = lax.all_to_all(pieces, 'req', 0, 0, tiled=True)  63.1 us
    psum x1, waiting for transfers between devices, body(): gate_full, up_full = lax.psum((gate_acts, up_acts), 'head')  24 us
    reshape x1, local copies, waits for them, and re-layouts, attend_pool(): key_rows = key_pool.reshape(pool_len, groups, HD)  11.1 us
    reshape x1, local copies, waits for them, and re-layouts, attend_pool(): value_rows = value_pool.reshape(pool_len, groups, HD)  11.1 us
    dot_general x1, matrix products, body(): down_acts = jnp.dot(hidden, down_weight, preferred_element_type=jnp.float32)  6.99 us
    dot_general x1, matrix products, attend_pool(): jnp.einsum('rgqt,tgd->rgqd', weights, value_rows, preferred_element_type=...  6.76 us
  transfers between devices with their start and end apart: 5, of which 5 were waited for; matrix products, arithmetic and copies ran while one was open for 0% of the time, Pallas kernels for 0%

profile of v1, /device:TPU:0, one launch (start us, length us, event | category | flops | bytes accessed | tf_op | source)
XLA Modules:
  0.0 310.3 jit_solution(6157071326091547463)
XLA Ops:
  6.5 0.7 broadcast_compare_fusion
  7.3 0.9 select_reduce_fusion.1
  8.2 0.9 fusion.24
  9.9 11.1 %reshape.86 = bf16[5888,4,128]{2,1,0:T(4,128)(2,1)} reshape(bf16[92,64,512]{2,1,0:T(8,128)(2,1)} %param.15) | data formatting | bytes 12058624 | tf_op jit(solution)/shard_map/reshape | solution.py:28
  21.3 5.2 %select_reduce_fusion = (f32[8,4,8]{2,0,1:T(8,128)S(1)}, f32[8,4,8,5888]{3,2,0,1:T(8,128)S(1)}) fusion(pred[8,5888]{1,0:T(8,128)(4,1)S(1)} %fusion.25, bf16[8,4,8,128]{3,0,2,1:T(8,128)(2,1)S(1)} %bitcast.56, bf16[5888,4,128,1]{2,1,0,3:T(4,128)(2,1)} %bitcast.50), kind=kOutput, calls=%fused_computation.8 | convolution fusion | flops 390397696 | bytes 12172288 | tf_op jit(solution)/shard_map/rgqd,tgd->rgqt/dot_general | solution.py:31
  26.5 2.6 copy-done.2
  29.1 1.5 fusion.4
  30.6 11.1 %reshape.89 = bf16[5888,4,128]{2,1,0:T(4,128)(2,1)} reshape(bf16[92,64,512]{2,1,0:T(8,128)(2,1)} %param.16) | data formatting | bytes 12058624 | tf_op jit(solution)/shard_map/reshape | solution.py:29
  41.7 6.8 %fusion.15 = bf16[8,4,8,128]{3,2,0,1:T(8,128)(2,1)S(1)} fusion(bf16[5888,4,128,1]{2,1,0,3:T(4,128)(2,1)} %bitcast.52, f32[8,4,8,5888]{3,2,0,1:T(8,128)} %copy-done.2, f32[8,4,8]{2,0,1:T(8,128)S(1)} %get-tuple-element.10, f32[8,4,8]{2,0,1:T(8,128)S(1)} %fusion.32, pred[8,5888]{1,0:T(8,128)(4,1)S(1)} %fusion.25, f32[8,4,128]{2,0,1:T(8,128)S(1)} %bitcast_convert_fusion, ...), kind=kOutput, calls=%fused_computation.17 | convolution fusion | flops 392003584 | bytes 12190720 | tf_op jit(solution)/shard_map/rgqt,tgd->rgqd/dot_general | solution.py:46
  48.5 0.7 copy.73
  49.4 1.9 collective-permute-done
  51.3 69.1 %all-gather.3.cloned.1.call-done = bf16[512,4096]{1,0:T(8,128)(2,1)} async-done(((bf16[8,4096]{1,0:T(8,128)(2,1)}), bf16[512,4096]{1,0:T(8,128)(2,1)}) %all-gather.3.cloned.1.call-update) | async-done | bytes 4194320 | tf_op jit(solution)/shard_map/all_gather | solution.py:80
  120.4 3.7 %fusion.18 = f32[512,128]{0,1:T(8,128)S(1)} fusion(bf16[512,4096]{1,0:T(8,128)(2,1)} %all-gather.3.cloned.1.call-done, bf16[4096,64]{0,1:T(8,128)(2,1)S(1)} %collective-permute-done, bf16[4096,64]{0,1:T(8,128)(2,1)S(1)} %get-tuple-element.7), kind=kOutput, calls=%fused_computation.18 | convolution fusion | flops 538968064 | bytes 5505024 | tf_op jit(solution)/shard_map/dot_general | solution.py:81
  124.2 1.3 collective-permute-done.1
  125.5 0.7 fusion.27
  126.5 65.9 %all-gather.5.cloned.1.call-done = bf16[512,4096]{0,1:T(8,128)(2,1)} async-done(((bf16[512,64]{0,1:T(8,128)(2,1)}), bf16[512,4096]{0,1:T(8,128)(2,1)}) %all-gather.5.cloned.1.call-update) | async-done | bytes 4194320 | tf_op jit(solution)/shard_map/all_gather | solution.py:88
  192.3 6.4 %fusion.38 = f32[512,448]{0,1:T(8,128)} fusion(bf16[4096,448]{0,1:T(8,128)(2,1)} %param.21, bf16[512,4096]{0,1:T(8,128)(2,1)} %all-gather.5.cloned.1.call-done), kind=kOutput, calls=%fused_computation.54 | convolution fusion | flops 1879048192 | bytes 8781824 | tf_op jit(solution)/shard_map/dot_general | solution.py:89
  198.7 3.0 fusion.39
  201.8 24.0 %all-reduce.3.cloned.1.call-done = (f32[512,448]{0,1:T(8,128)}, f32[512,448]{0,1:T(8,128)}) async-done(((f32[512,448]{0,1:T(8,128)}, f32[512,448]{0,1:T(8,128)}), (f32[512,448]{0,1:T(8,128)}, f32[512,448]{0,1:T(8,128)})) %all-reduce.3.cloned.1.call-update) | async-done | bytes 1835024 | tf_op jit(solution)/shard_map/psum | solution.py:91
  225.8 7.0 %convolution_convert_fusion = bf16[512,4096]{1,0:T(8,128)(2,1)} fusion(bf16[448,4096]{1,0:T(8,128)(2,1)} %param.23, f32[512,448]{0,1:T(8,128)} %get-tuple-element.5, f32[512,448]{0,1:T(8,128)} %get-tuple-element.6), kind=kOutput, calls=%fused_computation.9 | convolution fusion | flops 1882521600 | bytes 9699328 | tf_op jit(solution)/shard_map/dot_general | solution.py:93
  232.8 6.5 %copy.25 = bf16[512,4096]{0,1:T(8,128)(2,1)} copy(bf16[512,4096]{1,0:T(8,128)(2,1)} %convolution_convert_fusion) | data formatting | bytes 8388608 | tf_op jit(solution)/shard_map/convert_element_type | solution.py:96
  239.3 63.1 %all_to_all.5 = bf16[64,512,64]{1,2,0:T(8,128)(2,1)S(1)} all-to-all(bf16[64,512,64]{1,2,0:T(8,128)(2,1)} %bitcast.51), channel_id=1, replica_groups=mesh['head'=2,'req'=64] {'req'}, dimensions={0} | all-to-all | bytes 8388608 | tf_op jit(solution)/shard_map/all_to_all | solution.py:100
  302.3 0.6 convert_reduce_fusion
  303.2 0.6 add_convert_fusion
  (44 shorter events, 1.9 us)
Async XLA Ops:
  6.5 14.4 %copy-start = (bf16[8,512]{1,0:T(8,128)(2,1)S(1)}, bf16[8,512]{1,0:T(8,128)(2,1)}, u32[]{:S(2)}) copy-start(bf16[8,512]{1,0:T(8,128)(2,1)} %param.13) | copy-start | bytes 24580
  6.5 113.8 %all-gather.3.cloned.1.call-start = ((), (), s32[]{:S(2)}) async-start(), calls=%async_computation.1 | async-start | bytes 4259840 | tf_op jit(solution)/shard_map/all_gather | solution.py:80
  9.9 11.1 %copy-start.5 = (bf16[8,4096]{1,0:T(8,128)(2,1)S(1)}, bf16[8,4096]{1,0:T(8,128)(2,1)}, u32[]{:S(2)}) copy-start(bf16[8,4096]{1,0:T(8,128)(2,1)} %param.12) | copy-start | bytes 196612
  9.9 11.3 %copy-start.8 = (s32[8]{0:T(128)S(1)}, s32[8]{0:T(128)}, u32[]{:S(2)}) copy-start(s32[8]{0:T(128)} %param.17) | copy-start | bytes 100
  26.5 2.6 copy-start.2
  30.6 11.1 %copy-start.7 = (bf16[8,512]{1,0:T(8,128)(2,1)S(1)}, bf16[8,512]{1,0:T(8,128)(2,1)}, u32[]{:S(2)}) copy-start(bf16[8,512]{1,0:T(8,128)(2,1)} %param.14) | copy-start | bytes 24580
  41.7 7.5 %copy-start.3 = (bf16[8192,64]{0,1:T(8,128)(2,1)S(1)}, bf16[8192,64]{0,1:T(8,128)(2,1)}, u32[]{:S(2)}) copy-start(bf16[8192,64]{0,1:T(8,128)(2,1)} %param.20) | copy-start | bytes 3145732
  49.1 143.2 %all-gather.5.cloned.1.call-start = ((), (), s32[]{:S(2)}) async-start(), calls=%async_computation.2 | async-start | bytes 4259840 | tf_op jit(solution)/shard_map/all_gather | solution.py:88
  49.2 76.3 %copy-start.6 = (bf16[512,64]{0,1:T(8,128)(2,1)S(1)}, bf16[512,64]{0,1:T(8,128)(2,1)}, u32[]{:S(2)}) copy-start(bf16[512,64]{0,1:T(8,128)(2,1)} %param.19) | copy-start | bytes 196612
  49.3 2.0 collective-permute-start
  124.1 1.4 collective-permute-start.1
  126.2 99.5 %all-reduce.3.cloned.1.call-start = ((), (), s32[]{:S(2)}) async-start(), calls=%async_computation.3 | async-start | bytes 3670016 | tf_op jit(solution)/shard_map/psum | solution.py:91
  192.3 6.4 %copy-start.9 = (bf16[512,4096]{0,1:T(8,128)(2,1)S(1)}, bf16[512,4096]{0,1:T(8,128)(2,1)}, u32[]{:S(2)}) copy-start(bf16[512,4096]{0,1:T(8,128)(2,1)} %all-gather.5.cloned.1.call-done) | copy-start | bytes 12582916
  192.3 6.4 %copy-start.10 = (bf16[4096,448]{0,1:T(8,128)(2,1)S(1)}, bf16[4096,448]{0,1:T(8,128)(2,1)}, u32[]{:S(2)}) copy-start(bf16[4096,448]{0,1:T(8,128)(2,1)} %param.22) | copy-start | bytes 11010052
  239.2 64.6 %copy-start.1 = (bf16[8,512]{1,0:T(8,128)(2,1)S(1)}, bf16[8,512]{1,0:T(8,128)(2,1)}, u32[]{:S(2)}) copy-start(bf16[8,512]{1,0:T(8,128)(2,1)} %param.13) | copy-start | bytes 24580
  302.3 0.8 copy-start.4
Sparse Core Ops, SparseCore 0:
  49.3 71.0 all-gather.2
  126.3 65.9 all-gather.4
  201.9 23.8 all-reduce.2

commit v2 on v1

--- a/solution.py
+++ b/solution.py
@@ -50,6 +50,12 @@
     return summed.reshape(row_count, -1).astype(jnp.bfloat16)
 
 
+def gather_rows(block, n_req):
+    copies = jnp.broadcast_to(block[None], (n_req,) + block.shape)
+    gathered = lax.all_to_all(copies, "req", 0, 0, tiled=True)
+    return gathered.reshape(n_req * block.shape[0], *block.shape[1:])
+
+
 def body(
     queries,
     new_key,
@@ -77,7 +83,7 @@
     attention = attend_pool(
         queries, new_key, new_value, key_cache, value_cache, lengths, page_table
     )
-    features = lax.all_gather(attention, "req", axis=0, tiled=True)
+    features = gather_rows(attention, n_req)
     both = jnp.dot(
         features,
         jnp.concatenate([own_rows, lent_rows], axis=1),
@@ -85,10 +91,13 @@
     )
     attn_update = both[:, :cols] + lax.ppermute(both[:, cols:], "head", swap)
     mixed_rows = (residual.astype(jnp.float32) + attn_update).astype(jnp.bfloat16)
-    shard_piece = lax.all_gather(mixed_rows, "req", axis=1, tiled=True)
+    shard_piece = gather_rows(mixed_rows.T, n_req).reshape(n_req, *mixed_rows.T.shape)
+    shard_piece = shard_piece.transpose(2, 0, 1).reshape(mixed_rows.shape[0], -1)
     gate_acts = jnp.dot(shard_piece, gate_weight, preferred_element_type=jnp.float32)
     up_acts = jnp.dot(shard_piece, up_weight, preferred_element_type=jnp.float32)
-    gate_full, up_full = lax.psum((gate_acts, up_acts), "head")
+    acts = jnp.concatenate([gate_acts, up_acts], axis=1)
+    acts = acts + lax.ppermute(acts, "head", swap)
+    gate_full, up_full = jnp.split(acts, 2, axis=1)
     hidden = (jax.nn.silu(gate_full) * up_full).astype(jnp.bfloat16)
     down_acts = jnp.dot(hidden, down_weight, preferred_element_type=jnp.float32)
     tokens = down_acts.shape[0]

time: 311 us -> 261 us (0.84)
  waiting for transfers between devices: 162 us -> 56.7 us
  blocking collectives: 63.1 us -> 125 us
  between operations: 13.3 us -> 0.25 us
  starting transfers between devices: 0.44 us -> 12.2 us
  matrix products: 32.2 us -> 24.3 us
    all_gather x2 -> x0, waiting for transfers between devices: 135 us -> none  [the longest x1 69.1 us: body(): features = lax.all_gather(attention, 'req', axis=0, tiled=True)]
    all_to_all x0 -> x1, blocking collectives: none -> 66.7 us  [gather_rows(): gathered = lax.all_to_all(copies, 'req', 0, 0, tiled=True)]
    all_to_all x0 -> x1, waiting for transfers between devices: none -> 49.7 us  [gather_rows(): gathered = lax.all_to_all(copies, 'req', 0, 0, tiled=True)]
    psum x1 -> x0, waiting for transfers between devices: 24 us -> none  [body(): gate_full, up_full = lax.psum((gate_acts, up_acts), 'head')]
    all_to_all x0 -> x1, starting transfers between devices: none -> 11.9 us  [gather_rows(): gathered = lax.all_to_all(copies, 'req', 0, 0, tiled=True)]
    all_to_all x1, blocking collectives: 63.1 us -> 58.5 us  [body(): gathered = lax.all_to_all(pieces, 'req', 0, 0, tiled=True)]
    dot_general x1, matrix products: 6.42 us -> 2.05 us  [body(): jnp.dot(shard_piece, gate_weight, preferred_element_type=jnp.float32)]
    ppermute x0 -> x1, waiting for transfers between devices: none -> 3.77 us  [body(): acts = acts + lax.ppermute(acts, 'head', swap)]
  transfers between devices with their start and end apart: 5 -> 4, of which waited for: 5 -> 4; matrix products, arithmetic and copies ran while one was open for 0% -> 0% of each run, Pallas kernels for 0% -> 0%
where the time goes in v2:
time: 261 us; the launch traced here: 260 us
  blocking collectives  125 us (48%)
  waiting for transfers between devices  56.7 us (22%)
  local copies, waits for them, and re-layouts  35.2 us (13%)
  matrix products  24.3 us (9%)
  starting transfers between devices  12.2 us (5%)
  other arithmetic  6.06 us (2%)
    all_to_all x1, blocking collectives, gather_rows(): gathered = lax.all_to_all(copies, 'req', 0, 0, tiled=True)  66.7 us
    all_to_all x1, blocking collectives, body(): gathered = lax.all_to_all(pieces, 'req', 0, 0, tiled=True)  58.5 us
    all_to_all x1, waiting for transfers between devices, gather_rows(): gathered = lax.all_to_all(copies, 'req', 0, 0, tiled=True)  49.7 us
    all_to_all x1, starting transfers between devices, gather_rows(): gathered = lax.all_to_all(copies, 'req', 0, 0, tiled=True)  11.9 us
    reshape x1, local copies, waits for them, and re-layouts, attend_pool(): key_rows = key_pool.reshape(pool_len, groups, HD)  11.1 us
    reshape x1, local copies, waits for them, and re-layouts, attend_pool(): value_rows = value_pool.reshape(pool_len, groups, HD)  11.1 us
    dot_general x1, matrix products, attend_pool(): jnp.einsum('rgqt,tgd->rgqd', weights, value_rows, preferred_element_type=...  6.67 us
    convert_element_type x1, local copies, waits for them, and re-layouts, body(): down_acts.astype(jnp.bfloat16)  6.5 us
  transfers between devices with their start and end apart: 4, of which 4 were waited for; matrix products, arithmetic and copies ran while one was open for 0% of the time, Pallas kernels for 0%

profile of v2, /device:TPU:0, one launch (start us, length us, event | category | flops | bytes accessed | tf_op | source)
XLA Modules:
  0.0 259.9 jit_solution(614157885389765496)
XLA Ops:
  0.0 0.7 broadcast_compare_fusion
  0.7 0.9 select_reduce_fusion.1
  1.7 0.9 fusion.27
  3.3 11.1 %reshape.98 = bf16[5888,4,128]{2,1,0:T(4,128)(2,1)} reshape(bf16[92,64,512]{2,1,0:T(8,128)(2,1)} %param.15) | data formatting | bytes 12058624 | tf_op jit(solution)/shard_map/reshape | solution.py:28
  14.7 5.2 %select_reduce_fusion = (f32[8,4,8]{2,0,1:T(8,128)S(1)}, f32[8,4,8,5888]{3,2,0,1:T(8,128)S(1)}) fusion(pred[8,5888]{1,0:T(8,128)(4,1)S(1)} %fusion.28, bf16[8,4,8,128]{3,0,2,1:T(8,128)(2,1)S(1)} %bitcast.65, bf16[5888,4,128,1]{2,1,0,3:T(4,128)(2,1)} %bitcast.56), kind=kOutput, calls=%fused_computation.8 | convolution fusion | flops 390397696 | bytes 12172288 | tf_op jit(solution)/shard_map/rgqd,tgd->rgqt/dot_general | solution.py:31
  20.0 2.6 copy-done.2
  22.6 1.5 fusion.4
  24.1 11.1 %reshape.101 = bf16[5888,4,128]{2,1,0:T(4,128)(2,1)} reshape(bf16[92,64,512]{2,1,0:T(8,128)(2,1)} %param.16) | data formatting | bytes 12058624 | tf_op jit(solution)/shard_map/reshape | solution.py:29
  35.2 6.7 %fusion.17 = bf16[8,4,8,128]{3,2,0,1:T(8,128)(2,1)S(1)} fusion(bf16[5888,4,128,1]{2,1,0,3:T(4,128)(2,1)} %bitcast.58, f32[8,4,8,5888]{3,2,0,1:T(8,128)} %copy-done.2, f32[8,4,8]{2,0,1:T(8,128)S(1)} %get-tuple-element.8, f32[8,4,8]{2,0,1:T(8,128)S(1)} %fusion.35, pred[8,5888]{1,0:T(8,128)(4,1)S(1)} %fusion.28, f32[8,4,128]{2,0,1:T(8,128)S(1)} %bitcast_convert_fusion, ...), kind=kOutput, calls=%fused_computation.20 | convolution fusion | flops 392003584 | bytes 12190720 | tf_op jit(solution)/shard_map/rgqt,tgd->rgqd/dot_general | solution.py:46
  41.9 2.5 broadcast_in_dim.57
  44.4 11.9 %all-to-all-start = ((bf16[64,8,4096]{2,1,0:T(8,128)(2,1)}), bf16[64,8,4096]{2,1,0:T(8,128)(2,1)}, u32[]{:S(2)}, u32[]{:S(2)}) async-start(bf16[64,8,4096]{2,1,0:T(8,128)(2,1)} %broadcast_in_dim.57), calls=%async_computation | async-start | bytes 8388608 | tf_op jit(solution)/shard_map/all_to_all | solution.py:55
  56.5 1.9 collective-permute-done
  58.4 49.7 %all-to-all-done = bf16[64,8,4096]{2,1,0:T(8,128)(2,1)} async-done(((bf16[64,8,4096]{2,1,0:T(8,128)(2,1)}), bf16[64,8,4096]{2,1,0:T(8,128)(2,1)}, u32[]{:S(2)}, u32[]{:S(2)}) %all-to-all-start) | async-done | bytes 4194336 | tf_op jit(solution)/shard_map/all_to_all | solution.py:55
  108.1 3.7 %fusion.5 = f32[512,128]{0,1:T(8,128)S(1)} fusion(bf16[64,8,4096]{2,1,0:T(8,128)(2,1)} %all-to-all-done, bf16[4096,64]{0,1:T(8,128)(2,1)S(1)} %collective-permute-done, bf16[4096,64]{0,1:T(8,128)(2,1)S(1)} %get-tuple-element.5), kind=kOutput, calls=%fused_computation.11 | convolution fusion | flops 538968064 | bytes 5505024 | tf_op jit(solution)/shard_map/dot_general | solution.py:87
  112.0 1.3 collective-permute-done.1
  113.8 66.7 %all_to_all.15 = bf16[64,64,512]{2,1,0:T(8,128)(2,1)S(1)} all-to-all(bf16[64,64,512]{2,1,0:T(8,128)(2,1)S(1)} %broadcast_in_dim.58), channel_id=1, replica_groups=mesh['head'=2,'req'=64] {'req'}, dimensions={0} | all-to-all | bytes 8388608 | tf_op jit(solution)/shard_map/all_to_all | solution.py:55
  180.6 2.0 fusion.42
  182.7 2.0 fusion.43
  185.0 3.8 %collective-permute-done.2 = f32[512,896]{0,1:T(8,128)S(1)} collective-permute-done((f32[512,896]{0,1:T(8,128)S(1)}, f32[512,896]{0,1:T(8,128)S(1)}, u32[]{:S(2)}, u32[]{:S(2)}) %collective-permute-start.2) | collective-permute-done | bytes 1835040 | tf_op jit(solution)/shard_map/ppermute | solution.py:99
  189.2 4.4 %convolution_convert_fusion = bf16[512,4096]{1,0:T(8,128)(2,1)} fusion(bf16[448,4096]{1,0:T(8,128)(2,1)S(1)} %copy-done.10, f32[512,896]{0,1:T(8,128)S(1)} %fusion.41), kind=kOutput, calls=%fused_computation.9 | convolution fusion | flops 1882521600 | bytes 9699328 | tf_op jit(solution)/shard_map/dot_general | solution.py:102
  193.6 6.5 %copy.25 = bf16[512,4096]{0,1:T(8,128)(2,1)} copy(bf16[512,4096]{1,0:T(8,128)(2,1)} %convolution_convert_fusion) | data formatting | bytes 8388608 | tf_op jit(solution)/shard_map/convert_element_type | solution.py:105
  200.1 58.5 %all_to_all.16 = bf16[64,512,64]{1,2,0:T(8,128)(2,1)S(1)} all-to-all(bf16[64,512,64]{1,2,0:T(8,128)(2,1)} %bitcast.57), channel_id=1, replica_groups=mesh['head'=2,'req'=64] {'req'}, dimensions={0} | all-to-all | bytes 8388608 | tf_op jit(solution)/shard_map/all_to_all | solution.py:109
  258.6 0.6 convert_reduce_fusion
  259.2 0.6 add_convert_fusion
  (44 shorter events, 2.6 us)
Async XLA Ops:
  0.0 14.5 %copy-start = (bf16[8,512]{1,0:T(8,128)(2,1)S(1)}, bf16[8,512]{1,0:T(8,128)(2,1)}, u32[]{:S(2)}) copy-start(bf16[8,512]{1,0:T(8,128)(2,1)} %param.13) | copy-start | bytes 24580
  3.3 11.1 %copy-start.4 = (bf16[8,4096]{1,0:T(8,128)(2,1)S(1)}, bf16[8,4096]{1,0:T(8,128)(2,1)}, u32[]{:S(2)}) copy-start(bf16[8,4096]{1,0:T(8,128)(2,1)} %param.12) | copy-start | bytes 196612
  3.3 11.3 %copy-start.7 = (s32[8]{0:T(128)S(1)}, s32[8]{0:T(128)}, u32[]{:S(2)}) copy-start(s32[8]{0:T(128)} %param.17) | copy-start | bytes 100
  20.0 2.6 %copy-start.2 = (f32[8,4,8,5888]{3,2,0,1:T(8,128)}, f32[8,4,8,5888]{3,2,0,1:T(8,128)S(1)}, u32[]{:S(2)}) copy-start(f32[8,4,8,5888]{3,2,0,1:T(8,128)S(1)} %get-tuple-element.10) | copy-start | bytes 18087940
  24.1 11.1 %copy-start.6 = (bf16[8,512]{1,0:T(8,128)(2,1)S(1)}, bf16[8,512]{1,0:T(8,128)(2,1)}, u32[]{:S(2)}) copy-start(bf16[8,512]{1,0:T(8,128)(2,1)} %param.14) | copy-start | bytes 24580
  44.4 11.9 %copy-start.3 = (bf16[8192,64]{0,1:T(8,128)(2,1)S(1)}, bf16[8192,64]{0,1:T(8,128)(2,1)}, u32[]{:S(2)}) copy-start(bf16[8192,64]{0,1:T(8,128)(2,1)} %param.20) | copy-start | bytes 3145732
  44.4 63.7 %all-to-all-start = ((bf16[64,8,4096]{2,1,0:T(8,128)(2,1)}), bf16[64,8,4096]{2,1,0:T(8,128)(2,1)}, u32[]{:S(2)}, u32[]{:S(2)}) async-start(bf16[64,8,4096]{2,1,0:T(8,128)(2,1)} %broadcast_in_dim.57), calls=%async_computation | async-start | bytes 8388608 | tf_op jit(solution)/shard_map/all_to_all | solution.py:55
  56.3 57.0 %copy-start.5 = (bf16[512,64]{0,1:T(8,128)(2,1)S(1)}, bf16[512,64]{0,1:T(8,128)(2,1)}, u32[]{:S(2)}) copy-start(bf16[512,64]{0,1:T(8,128)(2,1)} %param.19) | copy-start | bytes 196612
  56.5 2.0 collective-permute-start
  111.9 1.4 collective-permute-start.1
  113.8 66.8 %copy-start.8 = (bf16[4096,448]{0,1:T(8,128)(2,1)S(1)}, bf16[4096,448]{0,1:T(8,128)(2,1)}, u32[]{:S(2)}) copy-start(bf16[4096,448]{0,1:T(8,128)(2,1)} %param.21) | copy-start | bytes 11010052
  180.6 2.1 copy-start.9
  184.7 4.4 %copy-start.10 = (bf16[448,4096]{1,0:T(8,128)(2,1)S(1)}, bf16[448,4096]{1,0:T(8,128)(2,1)}, u32[]{:S(2)}) copy-start(bf16[448,4096]{1,0:T(8,128)(2,1)} %param.23) | copy-start | bytes 11010052
  184.9 3.9 %collective-permute-start.2 = (f32[512,896]{0,1:T(8,128)S(1)}, f32[512,896]{0,1:T(8,128)S(1)}, u32[]{:S(2)}, u32[]{:S(2)}) collective-permute-start(f32[512,896]{0,1:T(8,128)S(1)} %pad_maximum_fusion), channel_id=1, source_target_pairs={{0,64},{64,0},{1,65},{65,1},{2,66},{66,2},{3,67},{67,3},{4,68},{68... | collective-permute-start | bytes 5505032 | tf_op jit(solution)/shard_map/ppermute | solution.py:99
  200.1 59.8 %copy-start.1 = (bf16[8,512]{1,0:T(8,128)(2,1)S(1)}, bf16[8,512]{1,0:T(8,128)(2,1)}, u32[]{:S(2)}) copy-start(bf16[8,512]{1,0:T(8,128)(2,1)} %param.13) | copy-start | bytes 24580

commit v3 on v2

--- a/solution.py
+++ b/solution.py
@@ -25,12 +25,16 @@
     live_mask = (owned[:, :, None] & (position < lengths[:, None, None])).reshape(row_count, pool_len)
     live_mask = live_mask[:, None, None, :]
 
-    key_rows = key_pool.reshape(pool_len, groups, HD)
-    value_rows = value_pool.reshape(pool_len, groups, HD)
+    key_rows = key_pool.reshape(pool_len, kv_width)
+    value_rows = value_pool.reshape(pool_len, kv_width)
     grouped = queries.reshape(row_count, groups, per_group, HD)
-    scores = jnp.einsum(
-        "rgqd,tgd->rgqt", grouped, key_rows, preferred_element_type=jnp.float32
-    ) * HD ** (-0.5)
+    group_eye = jnp.eye(groups, dtype=queries.dtype)
+    spread = (grouped[:, :, :, None, :] * group_eye[None, :, None, :, None]).reshape(
+        row_count * groups * per_group, kv_width
+    )
+    scores = lax.dot_general(
+        spread, key_rows, (((1,), (1,)), ((), ())), preferred_element_type=jnp.float32
+    ).reshape(row_count, groups, per_group, pool_len) * HD ** (-0.5)
     own_score = jnp.einsum(
         "rgqd,rgd->rgq",
         grouped,
@@ -43,7 +47,14 @@
     total_mass = jnp.sum(exp_terms, axis=3) + own_exp
     weights = (exp_terms / total_mass[..., None]).astype(jnp.bfloat16)
     own_weight = (own_exp / total_mass).astype(jnp.bfloat16)
-    summed = jnp.einsum("rgqt,tgd->rgqd", weights, value_rows, preferred_element_type=jnp.float32)
+    every = jnp.dot(
+        weights.reshape(row_count * groups * per_group, pool_len),
+        value_rows,
+        preferred_element_type=jnp.float32,
+    ).reshape(row_count, groups, per_group, groups, HD)
+    summed = jnp.sum(
+        every * group_eye.astype(jnp.float32)[None, :, None, :, None], axis=3
+    )
     summed = summed + own_weight.astype(jnp.float32)[..., None] * new_value.reshape(
         row_count, groups, 1, HD
     ).astype(jnp.float32)
@@ -99,13 +110,12 @@
     acts = acts + lax.ppermute(acts, "head", swap)
     gate_full, up_full = jnp.split(acts, 2, axis=1)
     hidden = (jax.nn.silu(gate_full) * up_full).astype(jnp.bfloat16)
-    down_acts = jnp.dot(hidden, down_weight, preferred_element_type=jnp.float32)
-    tokens = down_acts.shape[0]
-    pieces = (
-        down_acts.astype(jnp.bfloat16)
-        .reshape(tokens, n_req, down_acts.shape[1] // n_req)
-        .transpose(1, 0, 2)
-    )
+    pieces = jnp.einsum(
+        "tf,fnc->ntc",
+        hidden,
+        down_weight.reshape(down_weight.shape[0], n_req, down_weight.shape[1] // n_req),
+        preferred_element_type=jnp.float32,
+    ).astype(jnp.bfloat16)
     gathered = lax.all_to_all(pieces, "req", 0, 0, tiled=True)
     down_part = jnp.sum(gathered.astype(jnp.float32), axis=0)
     return (mixed_rows.astype(jnp.float32) + down_part).astype(jnp.bfloat16)

time: 261 us -> 239 us (0.916)
  local copies, waits for them, and re-layouts: 35.2 us -> 15.9 us
  matrix products: 24.3 us -> 21.5 us
    reshape x2 -> x0, local copies, waits for them, and re-layouts: 22.2 us -> none  [the longest x1 11.1 us: attend_pool(): key_rows = key_pool.reshape(pool_len, groups, HD)]
    dot_general x0 -> x1, local copies, waits for them, and re-layouts: none -> 8.57 us  [attend_pool(): jnp.dot(weights.reshape(row_count * groups * per_group, pool_len), value_...]
    convert_element_type x2 -> x1, local copies, waits for them, and re-layouts: 6.52 us -> 0.01 us  [attend_pool(): summed = summed + own_weight.astype(jnp.float32)[..., None] * new_value.r...]
    dot_general x3 -> x2, matrix products: 16.3 us -> 11.1 us  [the longest x1 6.27 us: attend_pool(): jnp.dot(weights.reshape(row_count * groups * per_group, pool_len), value_...]
where the time goes in v3:
time: 239 us
  blocking collectives  124 us (52%)
  waiting for transfers between devices  57 us (24%)
  matrix products  21.5 us (9%)
  local copies, waits for them, and re-layouts  15.9 us (7%)
  starting transfers between devices  12.2 us (5%)
  other arithmetic  7.47 us (3%)
    all_to_all x1, blocking collectives, gather_rows(): gathered = lax.all_to_all(copies, 'req', 0, 0, tiled=True)  66.3 us
    all_to_all x1, blocking collectives, body(): gathered = lax.all_to_all(pieces, 'req', 0, 0, tiled=True)  58.2 us
    all_to_all x1, waiting for transfers between devices, gather_rows(): gathered = lax.all_to_all(copies, 'req', 0, 0, tiled=True)  50 us
    all_to_all x1, starting transfers between devices, gather_rows(): gathered = lax.all_to_all(copies, 'req', 0, 0, tiled=True)  11.9 us
    dot_general x1, local copies, waits for them, and re-layouts, attend_pool(): jnp.dot(weights.reshape(row_count * groups * per_group, pool_len), value_...  8.57 us
    dot_general x1, matrix products, attend_pool(): jnp.dot(weights.reshape(row_count * groups * per_group, pool_len), value_...  6.27 us
    dot_general x1, matrix products, attend_pool(): lax.dot_general(spread, key_rows, (((1,), (1,)), ((), ())), preferred_ele...  4.78 us
  transfers between devices with their start and end apart: 4, of which 4 were waited for; matrix products, arithmetic and copies ran while one was open for 0% of the time, Pallas kernels for 0%

profile of v3, /device:TPU:0, one launch (start us, length us, event | category | flops | bytes accessed | tf_op | source)
XLA Modules:
  0.0 238.8 jit_solution(4781986356482212008)
XLA Ops:
  0.0 0.7 broadcast_compare_fusion
  0.7 0.9 select_reduce_fusion.1
  1.7 0.9 fusion.24
  3.4 0.8 copy.21
  4.4 0.8 fusion.25
  5.2 4.8 %select_reduce_fusion = (f32[8,4,8]{2,1,0:T(4,128)S(1)}, f32[8,4,8,5888]{3,2,1,0:T(8,128)S(1)}) fusion(pred[8,5888]{1,0:T(8,128)(4,1)S(1)} %fusion.25, bf16[5888,512,1,1]{1,0,3,2:T(8,128)(2,1)} %bitcast.74, bf16[4,4]{1,0:T(4,128)(2,1)S(1)} %fusion.35, bf16[8,4,8,128]{3,2,1,0:T(8,128)(2,1)S(1)} %copy.21), kind=kOutput, calls=%fused_computation.4 | convolution fusion | flops 1548156672 | bytes 12172320 | tf_op jit(solution)/shard_map/dot_general | solution.py:35
  10.0 2.6 %copy-done.2 = f32[8,4,8,5888]{3,2,1,0:T(8,128)} copy-done((f32[8,4,8,5888]{3,2,1,0:T(8,128)}, f32[8,4,8,5888]{3,2,1,0:T(8,128)S(1)}, u32[]{:S(2)}) %copy-start.2) | copy-done | bytes 6029336
  12.5 1.5 fusion
  14.1 8.6 %copy.22 = bf16[512,5888]{1,0:T(8,128)(2,1)} copy(bf16[512,5888]{0,1:T(8,128)(2,1)} %bitcast.65) | data formatting | bytes 12058624 | tf_op jit(solution)/shard_map/dot_general | solution.py:50
  22.7 6.3 %fusion.11 = f32[8,4,8,128]{3,2,1,0:T(8,128)S(1)} fusion(bf16[4,128,5888,1,1]{2,1,0,4,3:T(8,128)(2,1)} %bitcast.66, f32[8,4,8]{2,1,0:T(4,128)S(1)} %get-tuple-element.8, f32[8,4,8,5888]{3,2,1,0:T(8,128)} %copy-done.2, f32[8,4,8]{2,1,0:T(4,128)S(1)} %multiply_maximum_fusion, pred[8,5888]{1,0:T(8,128)(4,1)S(1)} %fusion.25, f32[4,4]{1,0:T(4,128)S(1)} %fusion.36), kind=kOutput, calls=%fused_computation.16 | convolution fusion | flops 1549762560 | bytes 12238912 | tf_op jit(solution)/shard_map/dot_general | solution.py:50
  29.1 2.5 %broadcast_in_dim.59 = bf16[64,8,4096]{2,1,0:T(8,128)(2,1)} broadcast(bf16[8,4096]{1,0:T(8,128)(2,1)S(1)} %bitcast.70), dimensions={1,2} | broadcast | bytes 4259840 | tf_op jit(solution)/shard_map/broadcast_in_dim | solution.py:65
  31.6 11.9 %all-to-all-start = ((bf16[64,8,4096]{2,1,0:T(8,128)(2,1)}), bf16[64,8,4096]{2,1,0:T(8,128)(2,1)}, u32[]{:S(2)}, u32[]{:S(2)}) async-start(bf16[64,8,4096]{2,1,0:T(8,128)(2,1)} %broadcast_in_dim.59), calls=%async_computation | async-start | bytes 8388608 | tf_op jit(solution)/shard_map/all_to_all | solution.py:66
  43.7 1.9 collective-permute-done
  45.6 50.0 %all-to-all-done = bf16[64,8,4096]{2,1,0:T(8,128)(2,1)} async-done(((bf16[64,8,4096]{2,1,0:T(8,128)(2,1)}), bf16[64,8,4096]{2,1,0:T(8,128)(2,1)}, u32[]{:S(2)}, u32[]{:S(2)}) %all-to-all-start) | async-done | bytes 4194336 | tf_op jit(solution)/shard_map/all_to_all | solution.py:66
  95.6 3.7 %fusion.1 = f32[512,128]{0,1:T(8,128)S(1)} fusion(bf16[64,8,4096]{2,1,0:T(8,128)(2,1)} %all-to-all-done, bf16[4096,64]{0,1:T(8,128)(2,1)S(1)} %collective-permute-done, bf16[4096,64]{0,1:T(8,128)(2,1)S(1)} %get-tuple-element.5), kind=kOutput, calls=%fused_computation.6 | convolution fusion | flops 538968064 | bytes 5505024 | tf_op jit(solution)/shard_map/dot_general | solution.py:98
  99.4 1.3 collective-permute-done.1
  101.3 66.3 %all_to_all.15 = bf16[64,64,512]{2,1,0:T(8,128)(2,1)S(1)} all-to-all(bf16[64,64,512]{2,1,0:T(8,128)(2,1)S(1)} %broadcast_in_dim.60), channel_id=1, replica_groups=mesh['head'=2,'req'=64] {'req'}, dimensions={0} | all-to-all | bytes 8388608 | tf_op jit(solution)/shard_map/all_to_all | solution.py:66
  167.6 2.0 fusion.41
  169.6 2.0 fusion.42
  171.9 3.8 %collective-permute-done.2 = f32[512,896]{0,1:T(8,128)S(1)} collective-permute-done((f32[512,896]{0,1:T(8,128)S(1)}, f32[512,896]{0,1:T(8,128)S(1)}, u32[]{:S(2)}, u32[]{:S(2)}) %collective-permute-start.2) | collective-permute-done | bytes 1835040 | tf_op jit(solution)/shard_map/ppermute | solution.py:110
  176.1 2.5 %fusion.18 = f32[512,4096]{0,1:S(1)} fusion(bf16[448,4096]{1,0:T(8,128)(2,1)S(1)} %copy-done.8, f32[512,896]{0,1:T(8,128)S(1)} %fusion.40), kind=kOutput, calls=%fused_computation.22 | convolution fusion | flops 1880424448 | bytes 13893632
  178.6 0.6 convert_bitcast_fusion
  179.3 58.2 %all_to_all.16 = bf16[64,512,64]{1,2,0:T(8,128)(2,1)S(1)} all-to-all(bf16[64,512,64]{1,2,0:T(8,128)(2,1)S(1)} %convert_bitcast_fusion), channel_id=1, replica_groups=mesh['head'=2,'req'=64] {'req'}, dimensions={0} | all-to-all | bytes 8388608 | tf_op jit(solution)/shard_map/all_to_all | solution.py:119
  238.1 0.6 add_convert_fusion
  (43 shorter events, 3.2 us)
Async XLA Ops:
  0.0 4.2 %copy-start = (bf16[8,512]{1,0:T(8,128)(2,1)S(1)}, bf16[8,512]{1,0:T(8,128)(2,1)}, u32[]{:S(2)}) copy-start(bf16[8,512]{1,0:T(8,128)(2,1)} %param.13) | copy-start | bytes 24580
  9.9 2.6 %copy-start.2 = (f32[8,4,8,5888]{3,2,1,0:T(8,128)}, f32[8,4,8,5888]{3,2,1,0:T(8,128)S(1)}, u32[]{:S(2)}) copy-start(f32[8,4,8,5888]{3,2,1,0:T(8,128)S(1)} %get-tuple-element.10) | copy-start | bytes 18087940
  14.1 8.6 %copy-start.5 = (bf16[8,512]{1,0:T(8,128)(2,1)S(1)}, bf16[8,512]{1,0:T(8,128)(2,1)}, u32[]{:S(2)}) copy-start(bf16[8,512]{1,0:T(8,128)(2,1)} %param.14) | copy-start | bytes 24580
  31.6 11.9 %copy-start.3 = (bf16[8192,64]{0,1:T(8,128)(2,1)S(1)}, bf16[8192,64]{0,1:T(8,128)(2,1)}, u32[]{:S(2)}) copy-start(bf16[8192,64]{0,1:T(8,128)(2,1)} %param.20) | copy-start | bytes 3145732
  31.6 64.0 %all-to-all-start = ((bf16[64,8,4096]{2,1,0:T(8,128)(2,1)}), bf16[64,8,4096]{2,1,0:T(8,128)(2,1)}, u32[]{:S(2)}, u32[]{:S(2)}) async-start(bf16[64,8,4096]{2,1,0:T(8,128)(2,1)} %broadcast_in_dim.59), calls=%async_computation | async-start | bytes 8388608 | tf_op jit(solution)/shard_map/all_to_all | solution.py:66
  43.5 57.2 %copy-start.4 = (bf16[512,64]{0,1:T(8,128)(2,1)S(1)}, bf16[512,64]{0,1:T(8,128)(2,1)}, u32[]{:S(2)}) copy-start(bf16[512,64]{0,1:T(8,128)(2,1)} %param.19) | copy-start | bytes 196612
  43.6 2.0 collective-permute-start
  99.3 1.4 collective-permute-start.1
  101.3 66.3 %copy-start.6 = (bf16[4096,448]{0,1:T(8,128)(2,1)S(1)}, bf16[4096,448]{0,1:T(8,128)(2,1)}, u32[]{:S(2)}) copy-start(bf16[4096,448]{0,1:T(8,128)(2,1)} %param.21) | copy-start | bytes 11010052
  167.6 2.1 copy-start.7
  171.7 4.4 %copy-start.8 = (bf16[448,4096]{1,0:T(8,128)(2,1)S(1)}, bf16[448,4096]{1,0:T(8,128)(2,1)}, u32[]{:S(2)}) copy-start(bf16[448,4096]{1,0:T(8,128)(2,1)} %param.23) | copy-start | bytes 11010052
  171.8 3.9 %collective-permute-start.2 = (f32[512,896]{0,1:T(8,128)S(1)}, f32[512,896]{0,1:T(8,128)S(1)}, u32[]{:S(2)}, u32[]{:S(2)}) collective-permute-start(f32[512,896]{0,1:T(8,128)S(1)} %pad_maximum_fusion), channel_id=1, source_target_pairs={{0,64},{64,0},{1,65},{65,1},{2,66},{66,2},{3,67},{67,3},{4,68},{68... | collective-permute-start | bytes 5505032 | tf_op jit(solution)/shard_map/ppermute | solution.py:110
  179.3 59.5 %copy-start.1 = (bf16[8,512]{1,0:T(8,128)(2,1)S(1)}, bf16[8,512]{1,0:T(8,128)(2,1)}, u32[]{:S(2)}) copy-start(bf16[8,512]{1,0:T(8,128)(2,1)} %param.13) | copy-start | bytes 24580

commit v4 on v3

--- a/solution.py
+++ b/solution.py
@@ -1,9 +1,31 @@
 import jax
 import jax.numpy as jnp
 from jax import lax
+from jax.experimental import pallas as pl
+from jax.experimental.pallas import tpu as pltpu
 from jax.sharding import PartitionSpec as P
 
 HD = 128
+INTERPRET = False
+
+
+def softmax_kernel(q_ref, k_ref, v_ref, live_ref, own_ref, out_ref, own_w_ref, w_scr):
+    rows_per_req = q_ref.shape[0] // live_ref.shape[0]
+    scores = lax.dot_general(
+        q_ref[...], k_ref[...], (((1,), (1,)), ((), ())), preferred_element_type=jnp.float32
+    ) * HD ** (-0.5)
+    for r in range(live_ref.shape[0]):
+        rows = slice(r * rows_per_req, (r + 1) * rows_per_req)
+        part = scores[rows, :]
+        live = live_ref[r : r + 1, :] != 0
+        own = own_ref[rows, :]
+        top = jnp.maximum(jnp.max(jnp.where(live, part, -1e30), axis=1, keepdims=True), own)
+        exp_terms = jnp.where(live, jnp.exp(part - top), 0.0)
+        own_exp = jnp.exp(own - top)
+        total = jnp.sum(exp_terms, axis=1, keepdims=True) + own_exp
+        w_scr[rows, :] = (exp_terms / total).astype(jnp.bfloat16)
+        own_w_ref[rows, :] = (own_exp / total).astype(jnp.bfloat16).astype(jnp.float32)
+    out_ref[...] = jnp.dot(w_scr[...], v_ref[...], preferred_element_type=jnp.float32)
 
 
 def attend_pool(queries, new_key, new_value, key_pool, value_pool, lengths, page_table):
@@ -23,7 +45,6 @@
     base = jnp.sum(jnp.where(match, slot_start[:, :, None], 0), axis=1)
     position = base[:, :, None] + lax.broadcasted_iota(jnp.int32, (1, 1, page_rows), 2)
     live_mask = (owned[:, :, None] & (position < lengths[:, None, None])).reshape(row_count, pool_len)
-    live_mask = live_mask[:, None, None, :]
 
     key_rows = key_pool.reshape(pool_len, kv_width)
     value_rows = value_pool.reshape(pool_len, kv_width)
@@ -32,30 +53,31 @@
     spread = (grouped[:, :, :, None, :] * group_eye[None, :, None, :, None]).reshape(
         row_count * groups * per_group, kv_width
     )
-    scores = lax.dot_general(
-        spread, key_rows, (((1,), (1,)), ((), ())), preferred_element_type=jnp.float32
-    ).reshape(row_count, groups, per_group, pool_len) * HD ** (-0.5)
     own_score = jnp.einsum(
         "rgqd,rgd->rgq",
         grouped,
         new_key.reshape(row_count, groups, HD),
         preferred_element_type=jnp.float32,
     ) * HD ** (-0.5)
-    top_score = jnp.maximum(jnp.max(jnp.where(live_mask, scores, -1e30), axis=3), own_score)
-    exp_terms = jnp.where(live_mask, jnp.exp(scores - top_score[..., None]), 0.0)
-    own_exp = jnp.exp(own_score - top_score)
-    total_mass = jnp.sum(exp_terms, axis=3) + own_exp
-    weights = (exp_terms / total_mass[..., None]).astype(jnp.bfloat16)
-    own_weight = (own_exp / total_mass).astype(jnp.bfloat16)
-    every = jnp.dot(
-        weights.reshape(row_count * groups * per_group, pool_len),
-        value_rows,
-        preferred_element_type=jnp.float32,
-    ).reshape(row_count, groups, per_group, groups, HD)
+    n_rows = row_count * groups * per_group
+    vmem = pl.BlockSpec(memory_space=pltpu.VMEM)
+    flat, own_w = pl.pallas_call(
+        softmax_kernel,
+        out_shape=(
+            jax.ShapeDtypeStruct((n_rows, kv_width), jnp.float32),
+            jax.ShapeDtypeStruct((n_rows, 1), jnp.float32),
+        ),
+        in_specs=[vmem] * 5,
+        out_specs=(vmem, vmem),
+        scratch_shapes=[pltpu.VMEM((n_rows, pool_len), jnp.bfloat16)],
+        interpret=INTERPRET,
+    )(spread, key_rows, value_rows, live_mask.astype(jnp.int32), own_score.reshape(n_rows, 1))
+    every = flat.reshape(row_count, groups, per_group, groups, HD)
+    own_weight = own_w.reshape(row_count, groups, per_group)
     summed = jnp.sum(
         every * group_eye.astype(jnp.float32)[None, :, None, :, None], axis=3
     )
-    summed = summed + own_weight.astype(jnp.float32)[..., None] * new_value.reshape(
+    summed = summed + own_weight[..., None] * new_value.reshape(
         row_count, groups, 1, HD
     ).astype(jnp.float32)
     return summed.reshape(row_count, -1).astype(jnp.bfloat16)

time: 239 us -> 232 us (0.971)
  matrix products: 21.5 us -> 10.5 us
  Pallas kernels: 0 us -> 11 us
  local copies, waits for them, and re-layouts: 15.9 us -> 5.6 us
  other arithmetic: 7.47 us -> 10.3 us
    dot_general x2 -> x0, matrix products: 11.1 us -> none  [the longest x1 6.27 us: attend_pool(): jnp.dot(weights.reshape(row_count * groups * per_group, pool_len), value_...]
    pallas_call x0 -> x1, Pallas kernels: none -> 11 us  [attend_pool(): pl.pallas_call(softmax_kernel, out_shape=(jax.ShapeDtypeStruct((n_rows, k...]
    dot_general x1 -> x0, local copies, waits for them, and re-layouts: 8.57 us -> none  [attend_pool(): jnp.dot(weights.reshape(row_count * groups * per_group, pool_len), value_...]
    unnamed x19 -> x15, local copies, waits for them, and re-layouts: 2.65 us -> 0.07 us
where the time goes in v4:
time: 232 us; the launch traced here: 231 us
  blocking collectives  124 us (53%)
  waiting for transfers between devices  57.2 us (25%)
  starting transfers between devices  12.2 us (5%)
  Pallas kernels  11 us (5%)
  matrix products  10.5 us (5%)
  other arithmetic  10.3 us (4%)
  local copies, waits for them, and re-layouts  5.6 us (2%)
    all_to_all x1, blocking collectives, gather_rows(): gathered = lax.all_to_all(copies, 'req', 0, 0, tiled=True)  65.9 us
    all_to_all x1, blocking collectives, body(): gathered = lax.all_to_all(pieces, 'req', 0, 0, tiled=True)  58.2 us
    all_to_all x1, waiting for transfers between devices, gather_rows(): gathered = lax.all_to_all(copies, 'req', 0, 0, tiled=True)  50.2 us
    all_to_all x1, starting transfers between devices, gather_rows(): gathered = lax.all_to_all(copies, 'req', 0, 0, tiled=True)  11.9 us
    pallas_call x1, Pallas kernels, attend_pool(): pl.pallas_call(softmax_kernel, out_shape=(jax.ShapeDtypeStruct((n_rows, k...  11 us
  transfers between devices with their start and end apart: 4, of which 4 were waited for; matrix products, arithmetic and copies ran while one was open for 0% of the time, Pallas kernels for 0%

profile of v4, /device:TPU:0, one launch (start us, length us, event | category | flops | bytes accessed | tf_op | source)
XLA Modules:
  0.0 231.1 jit_solution(11873828669908017917)
XLA Ops:
  0.0 0.7 broadcast_compare_fusion
  0.8 0.9 fusion.10
  1.7 0.9 select_reduce_fusion
  2.6 0.7 bitcast_convert_fusion
  3.4 0.8 copy.20
  4.8 0.8 reshape.123.own_ref
  5.5 0.8 broadcast_multiply_fusion
  6.6 1.4 fusion.12.live_ref
  8.1 11.0 %shard_map.118 = (f32[256,512]{1,0:T(8,128)}, f32[256,1]{1,0:T(8,128)}) custom-call(bf16[256,512]{1,0:T(8,128)(2,1)} %bitcast.44, bf16[5888,512]{1,0:T(8,128)(2,1)} %bitcast.40, bf16[5888,512]{1,0:T(8,128)(2,1)} %bitcast.41, s32[8,5888]{1,0:T(8,128)} %fusion.12.live_ref, f32[256,1]{1,0:T(8,128)} %reshape.123.own_ref), custom_call_target="tpu_custom_call" | custom-call | tf_op jit(solution)/shard_map/pallas_call | solution.py:64
  19.0 1.0 reduce
  20.1 1.2 multiply_reduce_fusion
  21.5 2.5 %broadcast_in_dim.18 = bf16[64,8,4096]{2,1,0:T(8,128)(2,1)} broadcast(bf16[8,4096]{1,0:T(8,128)(2,1)S(1)} %bitcast.47), dimensions={1,2} | broadcast | bytes 4259840 | tf_op jit(solution)/shard_map/broadcast_in_dim | solution.py:87
  23.9 11.9 %all-to-all-start = ((bf16[64,8,4096]{2,1,0:T(8,128)(2,1)}), bf16[64,8,4096]{2,1,0:T(8,128)(2,1)}, u32[]{:S(2)}, u32[]{:S(2)}) async-start(bf16[64,8,4096]{2,1,0:T(8,128)(2,1)} %broadcast_in_dim.18), calls=%async_computation | async-start | bytes 8388608 | tf_op jit(solution)/shard_map/all_to_all | solution.py:88
  36.1 1.9 collective-permute-done
  38.0 50.2 %all-to-all-done = bf16[64,8,4096]{2,1,0:T(8,128)(2,1)} async-done(((bf16[64,8,4096]{2,1,0:T(8,128)(2,1)}), bf16[64,8,4096]{2,1,0:T(8,128)(2,1)}, u32[]{:S(2)}, u32[]{:S(2)}) %all-to-all-start) | async-done | bytes 4194336 | tf_op jit(solution)/shard_map/all_to_all | solution.py:88
  88.2 3.7 %fusion = f32[512,128]{0,1:T(8,128)S(1)} fusion(bf16[64,8,4096]{2,1,0:T(8,128)(2,1)} %all-to-all-done, bf16[4096,64]{0,1:T(8,128)(2,1)S(1)} %collective-permute-done, bf16[4096,64]{0,1:T(8,128)(2,1)S(1)} %get-tuple-element.9), kind=kOutput, calls=%fused_computation.1 | convolution fusion | flops 538968064 | bytes 5505024 | tf_op jit(solution)/shard_map/dot_general | solution.py:120
  92.0 1.3 collective-permute-done.1
  93.9 65.9 %all_to_all.15 = bf16[64,64,512]{2,1,0:T(8,128)(2,1)S(1)} all-to-all(bf16[64,64,512]{2,1,0:T(8,128)(2,1)S(1)} %broadcast_in_dim.19), channel_id=1, replica_groups=mesh['head'=2,'req'=64] {'req'}, dimensions={0} | all-to-all | bytes 8388608 | tf_op jit(solution)/shard_map/all_to_all | solution.py:88
  159.8 2.0 fusion.23
  161.9 2.0 fusion.24
  164.2 3.8 %collective-permute-done.2 = f32[512,896]{0,1:T(8,128)S(1)} collective-permute-done((f32[512,896]{0,1:T(8,128)S(1)}, f32[512,896]{0,1:T(8,128)S(1)}, u32[]{:S(2)}, u32[]{:S(2)}) %collective-permute-start.2) | collective-permute-done | bytes 1835040 | tf_op jit(solution)/shard_map/ppermute | solution.py:132
  168.4 2.5 %fusion.6 = f32[512,4096]{0,1:S(1)} fusion(bf16[448,4096]{1,0:T(8,128)(2,1)S(1)} %copy-done.6, f32[512,896]{0,1:T(8,128)S(1)} %fusion.22), kind=kOutput, calls=%fused_computation.11 | convolution fusion | flops 1880424448 | bytes 13893632
  171.6 58.2 %all_to_all.16 = bf16[64,512,64]{1,2,0:T(8,128)(2,1)S(1)} all-to-all(bf16[64,512,64]{1,2,0:T(8,128)(2,1)S(1)} %convert_bitcast_fusion), channel_id=1, replica_groups=mesh['head'=2,'req'=64] {'req'}, dimensions={0} | all-to-all | bytes 8388608 | tf_op jit(solution)/shard_map/all_to_all | solution.py:141
  230.4 0.6 add_convert_fusion
  (40 shorter events, 3.9 us)
Async XLA Ops:
  0.0 4.2 %copy-start = (bf16[8,512]{1,0:T(8,128)(2,1)S(1)}, bf16[8,512]{1,0:T(8,128)(2,1)}, u32[]{:S(2)}) copy-start(bf16[8,512]{1,0:T(8,128)(2,1)} %param.13) | copy-start | bytes 24580
  23.9 11.9 %copy-start.2 = (bf16[8192,64]{0,1:T(8,128)(2,1)S(1)}, bf16[8192,64]{0,1:T(8,128)(2,1)}, u32[]{:S(2)}) copy-start(bf16[8192,64]{0,1:T(8,128)(2,1)} %param.20) | copy-start | bytes 3145732
  23.9 64.2 %all-to-all-start = ((bf16[64,8,4096]{2,1,0:T(8,128)(2,1)}), bf16[64,8,4096]{2,1,0:T(8,128)(2,1)}, u32[]{:S(2)}, u32[]{:S(2)}) async-start(bf16[64,8,4096]{2,1,0:T(8,128)(2,1)} %broadcast_in_dim.18), calls=%async_computation | async-start | bytes 8388608 | tf_op jit(solution)/shard_map/all_to_all | solution.py:88
  36.0 57.4 %copy-start.3 = (bf16[512,64]{0,1:T(8,128)(2,1)S(1)}, bf16[512,64]{0,1:T(8,128)(2,1)}, u32[]{:S(2)}) copy-start(bf16[512,64]{0,1:T(8,128)(2,1)} %param.19) | copy-start | bytes 196612
  36.0 2.0 collective-permute-start
  91.9 1.4 collective-permute-start.1
  93.9 66.0 %copy-start.4 = (bf16[4096,448]{0,1:T(8,128)(2,1)S(1)}, bf16[4096,448]{0,1:T(8,128)(2,1)}, u32[]{:S(2)}) copy-start(bf16[4096,448]{0,1:T(8,128)(2,1)} %param.21) | copy-start | bytes 11010052
  159.8 2.1 copy-start.5
  164.1 4.3 %copy-start.6 = (bf16[448,4096]{1,0:T(8,128)(2,1)S(1)}, bf16[448,4096]{1,0:T(8,128)(2,1)}, u32[]{:S(2)}) copy-start(bf16[448,4096]{1,0:T(8,128)(2,1)} %param.23) | copy-start | bytes 11010052
  164.1 3.9 %collective-permute-start.2 = (f32[512,896]{0,1:T(8,128)S(1)}, f32[512,896]{0,1:T(8,128)S(1)}, u32[]{:S(2)}, u32[]{:S(2)}) collective-permute-start(f32[512,896]{0,1:T(8,128)S(1)} %pad_maximum_fusion), channel_id=1, source_target_pairs={{0,64},{64,0},{1,65},{65,1},{2,66},{66,2},{3,67},{67,3},{4,68},{68... | collective-permute-start | bytes 5505032 | tf_op jit(solution)/shard_map/ppermute | solution.py:132
  171.6 59.5 %copy-start.1 = (bf16[8,512]{1,0:T(8,128)(2,1)S(1)}, bf16[8,512]{1,0:T(8,128)(2,1)}, u32[]{:S(2)}) copy-start(bf16[8,512]{1,0:T(8,128)(2,1)} %param.13) | copy-start | bytes 24580

commit v5 on v4

--- a/solution.py
+++ b/solution.py
@@ -10,22 +10,26 @@
 
 
 def softmax_kernel(q_ref, k_ref, v_ref, live_ref, own_ref, out_ref, own_w_ref, w_scr):
-    rows_per_req = q_ref.shape[0] // live_ref.shape[0]
-    scores = lax.dot_general(
-        q_ref[...], k_ref[...], (((1,), (1,)), ((), ())), preferred_element_type=jnp.float32
-    ) * HD ** (-0.5)
-    for r in range(live_ref.shape[0]):
-        rows = slice(r * rows_per_req, (r + 1) * rows_per_req)
-        part = scores[rows, :]
-        live = live_ref[r : r + 1, :] != 0
-        own = own_ref[rows, :]
-        top = jnp.maximum(jnp.max(jnp.where(live, part, -1e30), axis=1, keepdims=True), own)
-        exp_terms = jnp.where(live, jnp.exp(part - top), 0.0)
-        own_exp = jnp.exp(own - top)
-        total = jnp.sum(exp_terms, axis=1, keepdims=True) + own_exp
-        w_scr[rows, :] = (exp_terms / total).astype(jnp.bfloat16)
-        own_w_ref[rows, :] = (own_exp / total).astype(jnp.bfloat16).astype(jnp.float32)
-    out_ref[...] = jnp.dot(w_scr[...], v_ref[...], preferred_element_type=jnp.float32)
+    groups, rows, _ = q_ref.shape
+    requests = live_ref.shape[0]
+    per_req = rows // requests
+    for g in range(groups):
+        cols = slice(g * HD, (g + 1) * HD)
+        scores = lax.dot_general(
+            q_ref[g], k_ref[:, cols], (((1,), (1,)), ((), ())), preferred_element_type=jnp.float32
+        ) * HD ** (-0.5)
+        for r in range(requests):
+            part_rows = slice(r * per_req, (r + 1) * per_req)
+            part = scores[part_rows, :]
+            live = live_ref[r : r + 1, :] != 0
+            own = own_ref[g, part_rows, :]
+            top = jnp.maximum(jnp.max(jnp.where(live, part, -1e30), axis=1, keepdims=True), own)
+            exp_terms = jnp.where(live, jnp.exp(part - top), 0.0)
+            own_exp = jnp.exp(own - top)
+            total = jnp.sum(exp_terms, axis=1, keepdims=True) + own_exp
+            w_scr[part_rows, :] = (exp_terms / total).astype(jnp.bfloat16)
+            own_w_ref[g, part_rows, :] = (own_exp / total).astype(jnp.bfloat16).astype(jnp.float32)
+        out_ref[g] = jnp.dot(w_scr[...], v_ref[:, cols], preferred_element_type=jnp.float32)
 
 
 def attend_pool(queries, new_key, new_value, key_pool, value_pool, lengths, page_table):
@@ -49,34 +53,33 @@
     key_rows = key_pool.reshape(pool_len, kv_width)
     value_rows = value_pool.reshape(pool_len, kv_width)
     grouped = queries.reshape(row_count, groups, per_group, HD)
-    group_eye = jnp.eye(groups, dtype=queries.dtype)
-    spread = (grouped[:, :, :, None, :] * group_eye[None, :, None, :, None]).reshape(
-        row_count * groups * per_group, kv_width
-    )
     own_score = jnp.einsum(
-        "rgqd,rgd->rgq",
+        "rgqd,rgd->grq",
         grouped,
         new_key.reshape(row_count, groups, HD),
         preferred_element_type=jnp.float32,
     ) * HD ** (-0.5)
-    n_rows = row_count * groups * per_group
+    by_group = grouped.transpose(1, 0, 2, 3).reshape(groups, row_count * per_group, HD)
     vmem = pl.BlockSpec(memory_space=pltpu.VMEM)
-    flat, own_w = pl.pallas_call(
+    summed, own_w = pl.pallas_call(
         softmax_kernel,
         out_shape=(
-            jax.ShapeDtypeStruct((n_rows, kv_width), jnp.float32),
-            jax.ShapeDtypeStruct((n_rows, 1), jnp.float32),
+            jax.ShapeDtypeStruct((groups, row_count * per_group, HD), jnp.float32),
+            jax.ShapeDtypeStruct((groups, row_count * per_group, 1), jnp.float32),
         ),
         in_specs=[vmem] * 5,
         out_specs=(vmem, vmem),
-        scratch_shapes=[pltpu.VMEM((n_rows, pool_len), jnp.bfloat16)],
+        scratch_shapes=[pltpu.VMEM((row_count * per_group, pool_len), jnp.bfloat16)],
         interpret=INTERPRET,
-    )(spread, key_rows, value_rows, live_mask.astype(jnp.int32), own_score.reshape(n_rows, 1))
-    every = flat.reshape(row_count, groups, per_group, groups, HD)
-    own_weight = own_w.reshape(row_count, groups, per_group)
-    summed = jnp.sum(
-        every * group_eye.astype(jnp.float32)[None, :, None, :, None], axis=3
+    )(
+        by_group,
+        key_rows,
+        value_rows,
+        live_mask.astype(jnp.int32),
+        own_score.reshape(groups, row_count * per_group, 1),
     )
+    summed = summed.reshape(groups, row_count, per_group, HD).transpose(1, 0, 2, 3)
+    own_weight = own_w.reshape(groups, row_count, per_group).transpose(1, 0, 2)
     summed = summed + own_weight[..., None] * new_value.reshape(
         row_count, groups, 1, HD
     ).astype(jnp.float32)
@@ -128,10 +131,21 @@
     shard_piece = shard_piece.transpose(2, 0, 1).reshape(mixed_rows.shape[0], -1)
     gate_acts = jnp.dot(shard_piece, gate_weight, preferred_element_type=jnp.float32)
     up_acts = jnp.dot(shard_piece, up_weight, preferred_element_type=jnp.float32)
-    acts = jnp.concatenate([gate_acts, up_acts], axis=1)
-    acts = acts + lax.ppermute(acts, "head", swap)
-    gate_full, up_full = jnp.split(acts, 2, axis=1)
-    hidden = (jax.nn.silu(gate_full) * up_full).astype(jnp.bfloat16)
+    units = gate_acts.shape[1] // 2
+    gate_parts = gate_acts.reshape(gate_acts.shape[0], 2, units)
+    up_parts = up_acts.reshape(up_acts.shape[0], 2, units)
+    own_part = jnp.concatenate(
+        [jnp.take(gate_parts, head, axis=1), jnp.take(up_parts, head, axis=1)], axis=1
+    )
+    lent_part = jnp.concatenate(
+        [jnp.take(gate_parts, 1 - head, axis=1), jnp.take(up_parts, 1 - head, axis=1)], axis=1
+    )
+    acts = own_part + lax.ppermute(lent_part, "head", swap)
+    gate_half, up_half = jnp.split(acts, 2, axis=1)
+    hidden_half = (jax.nn.silu(gate_half) * up_half).astype(jnp.bfloat16)
+    other_half = lax.ppermute(hidden_half, "head", swap)
+    halves = jnp.where(head == 0, jnp.stack([hidden_half, other_half]), jnp.stack([other_half, hidden_half]))
+    hidden = halves.transpose(1, 0, 2).reshape(hidden_half.shape[0], -1)
     pieces = jnp.einsum(
         "tf,fnc->ntc",
         hidden,

time: 232 us -> 250 us (1.078)
  blocking collectives: 124 us -> 64.6 us
  waiting for transfers between devices: 57.2 us -> 111 us
  starting transfers between devices: 12.2 us -> 26.6 us
  matrix products: 10.5 us -> 16.9 us
  local copies, waits for them, and re-layouts: 5.6 us -> 8.19 us
    all_to_all x1 -> x0, blocking collectives: 65.9 us -> none  [gather_rows(): gathered = lax.all_to_all(copies, 'req', 0, 0, tiled=True)]
    all_to_all x1 -> x2, waiting for transfers between devices: 50.2 us -> 104 us  [gather_rows(): gathered = lax.all_to_all(copies, 'req', 0, 0, tiled=True)]
    all_to_all x1 -> x2, starting transfers between devices: 11.9 us -> 26.2 us  [gather_rows(): gathered = lax.all_to_all(copies, 'req', 0, 0, tiled=True)]
    all_to_all x1, blocking collectives: 58.2 us -> 64.6 us  [body(): gathered = lax.all_to_all(pieces, 'req', 0, 0, tiled=True)]
    dot_general x1, matrix products: 2.05 us -> 5.5 us  [body(): jnp.dot(shard_piece, up_weight, preferred_element_type=jnp.float32)]
  transfers between devices with their start and end apart: 4 -> 6, of which waited for: 4 -> 6; matrix products, arithmetic and copies ran while one was open for 0% -> 0% of each run, Pallas kernels for 0% -> 0%
where the time goes in v5:
time: 250 us; the launch traced here: 249 us
  waiting for transfers between devices  111 us (44%)
  blocking collectives  64.6 us (26%)
  starting transfers between devices  26.6 us (11%)
  matrix products  16.9 us (7%)
  Pallas kernels  11.9 us (5%)
  other arithmetic  9.46 us (4%)
  local copies, waits for them, and re-layouts  8.19 us (3%)
    all_to_all x2, waiting for transfers between devices, gather_rows(): gathered = lax.all_to_all(copies, 'req', 0, 0, tiled=True)  104 us
    all_to_all x1, blocking collectives, body(): gathered = lax.all_to_all(pieces, 'req', 0, 0, tiled=True)  64.6 us
    all_to_all x2, starting transfers between devices, gather_rows(): gathered = lax.all_to_all(copies, 'req', 0, 0, tiled=True)  26.2 us
    pallas_call x1, Pallas kernels, attend_pool(): pl.pallas_call(softmax_kernel, out_shape=(jax.ShapeDtypeStruct((groups, r...  11.9 us
    dot_general x1, matrix products, body(): jnp.dot(shard_piece, up_weight, preferred_element_type=jnp.float32)  5.5 us
  transfers between devices with their start and end apart: 6, of which 6 were waited for; matrix products, arithmetic and copies ran while one was open for 0% of the time, Pallas kernels for 0%

profile of v5, /device:TPU:0, one launch (start us, length us, event | category | flops | bytes accessed | tf_op | source)
XLA Modules:
  0.0 249.1 jit_solution(12671955715788849113)
XLA Ops:
  0.7 0.9 fusion.7
  1.6 0.9 select_reduce_fusion
  2.6 1.5 copy.49
  4.1 1.0 fusion.14
  6.2 0.8 reshape.207.own_ref
  7.3 1.4 fusion.9.live_ref
  8.7 11.9 %shard_map.118 = (f32[4,64,128]{2,1,0:T(8,128)}, f32[4,64,1]{2,1,0:T(8,128)}) custom-call(bf16[4,64,128]{2,1,0:T(8,128)(2,1)} %bitcast.80, bf16[5888,512]{1,0:T(8,128)(2,1)} %bitcast.76, bf16[5888,512]{1,0:T(8,128)(2,1)} %bitcast.77, s32[8,5888]{1,0:T(8,128)} %fusion.9.live_ref, f32[4,64,1]{2,1,0:T(8,128)} %reshape.207.own_ref), custom_call_target="tpu_custom_call" | custom-call | tf_op jit(solution)/shard_map/pallas_call | solution.py:64
  20.6 1.0 reduce
  21.7 1.0 fusion.13
  22.8 2.5 broadcast_in_dim.24
  25.3 11.9 %all-to-all-start = ((bf16[64,8,4096]{2,1,0:T(8,128)(2,1)}), bf16[64,8,4096]{2,1,0:T(8,128)(2,1)}, u32[]{:S(2)}, u32[]{:S(2)}) async-start(bf16[64,8,4096]{2,1,0:T(8,128)(2,1)} %broadcast_in_dim.24), calls=%async_computation | async-start | bytes 8388608 | tf_op jit(solution)/shard_map/all_to_all | solution.py:91
  37.4 1.9 collective-permute-done
  39.3 50.1 %all-to-all-done = bf16[64,8,4096]{2,1,0:T(8,128)(2,1)} async-done(((bf16[64,8,4096]{2,1,0:T(8,128)(2,1)}), bf16[64,8,4096]{2,1,0:T(8,128)(2,1)}, u32[]{:S(2)}, u32[]{:S(2)}) %all-to-all-start) | async-done | bytes 4194336 | tf_op jit(solution)/shard_map/all_to_all | solution.py:91
  89.4 3.7 %fusion = f32[512,128]{0,1:T(8,128)S(1)} fusion(bf16[64,8,4096]{2,1,0:T(8,128)(2,1)} %all-to-all-done, bf16[4096,64]{0,1:T(8,128)(2,1)S(1)} %collective-permute-done, bf16[4096,64]{0,1:T(8,128)(2,1)S(1)} %get-tuple-element.21), kind=kOutput, calls=%fused_computation.1 | convolution fusion | flops 538968064 | bytes 5505024 | tf_op jit(solution)/shard_map/dot_general | solution.py:123
  93.3 1.3 collective-permute-done.1
  94.6 2.5 broadcast_in_dim.25
  97.1 14.2 %all-to-all-start.1 = ((bf16[64,64,512]{2,1,0:T(8,128)(2,1)}), bf16[64,64,512]{2,1,0:T(8,128)(2,1)}, u32[]{:S(2)}, u32[]{:S(2)}) async-start(bf16[64,64,512]{2,1,0:T(8,128)(2,1)} %broadcast_in_dim.25), calls=%async_computation.1 | async-start | bytes 8388608 | tf_op jit(solution)/shard_map/all_to_all | solution.py:91
  111.4 54.1 %all-to-all-done.1 = bf16[64,64,512]{2,1,0:T(8,128)(2,1)} async-done(((bf16[64,64,512]{2,1,0:T(8,128)(2,1)}), bf16[64,64,512]{2,1,0:T(8,128)(2,1)}, u32[]{:S(2)}, u32[]{:S(2)}) %all-to-all-start.1) | async-done | bytes 4194336 | tf_op jit(solution)/shard_map/all_to_all | solution.py:91
  165.5 5.5 %fusion.19 = f32[512,2,224]{0,2,1:T(8,128)S(1)} fusion(bf16[512,4096,1]{0,1,2:T(8,128)(2,1)} %bitcast.17, bf16[2,224,4096]{2,1,0:T(8,128)(2,1)} %bitcast.87), kind=kOutput, calls=%fused_computation.43 | convolution fusion | flops 1879048192 | bytes 8781824 | tf_op jit(solution)/shard_map/dot_general | solution.py:133
  171.0 4.2 %fusion.18 = f32[512,2,224]{0,2,1:T(8,128)S(1)} fusion(bf16[512,4096,1]{0,1,2:T(8,128)(2,1)} %bitcast.17, bf16[2,224,4096]{2,1,0:T(8,128)(2,1)S(1)} %bitcast.88), kind=kOutput, calls=%fused_computation.42 | convolution fusion | flops 1879048192 | bytes 8781824 | tf_op jit(solution)/shard_map/dot_general | solution.py:132
  175.6 2.4 collective-permute-done.2
  178.7 1.2 collective-permute-done.3
  180.0 2.5 fusion.20
  183.2 64.6 %all_to_all.15 = bf16[64,512,64]{1,2,0:T(8,128)(2,1)S(1)} all-to-all(bf16[64,512,64]{1,2,0:T(8,128)(2,1)S(1)} %convert_bitcast_fusion), channel_id=1, replica_groups=mesh['head'=2,'req'=64] {'req'}, dimensions={0} | all-to-all | bytes 8388608 | tf_op jit(solution)/shard_map/all_to_all | solution.py:155
  (42 shorter events, 5.7 us)
Async XLA Ops:
  0.0 4.1 %copy-start = (bf16[8,512]{1,0:T(8,128)(2,1)S(1)}, bf16[8,512]{1,0:T(8,128)(2,1)}, u32[]{:S(2)}) copy-start(bf16[8,512]{1,0:T(8,128)(2,1)} %param.15) | copy-start | bytes 24580
  25.3 11.9 %copy-start.3 = (bf16[8192,64]{0,1:T(8,128)(2,1)S(1)}, bf16[8192,64]{0,1:T(8,128)(2,1)}, u32[]{:S(2)}) copy-start(bf16[8192,64]{0,1:T(8,128)(2,1)} %param.22) | copy-start | bytes 3145732
  25.3 64.2 %all-to-all-start = ((bf16[64,8,4096]{2,1,0:T(8,128)(2,1)}), bf16[64,8,4096]{2,1,0:T(8,128)(2,1)}, u32[]{:S(2)}, u32[]{:S(2)}) async-start(bf16[64,8,4096]{2,1,0:T(8,128)(2,1)} %broadcast_in_dim.24), calls=%async_computation | async-start | bytes 8388608 | tf_op jit(solution)/shard_map/all_to_all | solution.py:91
  37.2 57.4 %copy-start.4 = (bf16[512,64]{0,1:T(8,128)(2,1)S(1)}, bf16[512,64]{0,1:T(8,128)(2,1)}, u32[]{:S(2)}) copy-start(bf16[512,64]{0,1:T(8,128)(2,1)} %param.21) | copy-start | bytes 196612
  37.3 2.0 collective-permute-start
  93.2 1.4 collective-permute-start.1
  97.1 68.3 %all-to-all-start.1 = ((bf16[64,64,512]{2,1,0:T(8,128)(2,1)}), bf16[64,64,512]{2,1,0:T(8,128)(2,1)}, u32[]{:S(2)}, u32[]{:S(2)}) async-start(bf16[64,64,512]{2,1,0:T(8,128)(2,1)} %broadcast_in_dim.25), calls=%async_computation.1 | async-start | bytes 8388608 | tf_op jit(solution)/shard_map/all_to_all | solution.py:91
  165.5 5.5 %copy-start.5 = (bf16[4096,448]{0,1:T(8,128)(2,1)S(1)}, bf16[4096,448]{0,1:T(8,128)(2,1)}, u32[]{:S(2)}) copy-start(bf16[4096,448]{0,1:T(8,128)(2,1)} %param.23) | copy-start | bytes 11010052
  175.5 2.6 %collective-permute-start.2 = (f32[512,448]{0,1:T(8,128)S(1)}, f32[512,448]{0,1:T(8,128)S(1)}, u32[]{:S(2)}, u32[]{:S(2)}) collective-permute-start(f32[512,448]{0,1:T(8,128)S(1)} %pad_maximum_fusion), channel_id=1, source_target_pairs={{0,64},{64,0},{1,65},{65,1},{2,66},{66,2},{3,67},{67,3},{4,68},{68... | collective-permute-start | bytes 2752520 | tf_op jit(solution)/shard_map/ppermute | solution.py:143
  175.6 4.4 %copy-start.2 = (bf16[448,4096]{1,0:T(8,128)(2,1)S(1)}, bf16[448,4096]{1,0:T(8,128)(2,1)}, u32[]{:S(2)}) copy-start(bf16[448,4096]{1,0:T(8,128)(2,1)} %param.25) | copy-start | bytes 11010052
  178.4 1.6 collective-permute-start.3
  183.1 65.9 %copy-start.1 = (bf16[8,512]{1,0:T(8,128)(2,1)S(1)}, bf16[8,512]{1,0:T(8,128)(2,1)}, u32[]{:S(2)}) copy-start(bf16[8,512]{1,0:T(8,128)(2,1)} %param.15) | copy-start | bytes 24580

commit v6 on v4

--- a/solution.py
+++ b/solution.py
@@ -10,22 +10,24 @@
 
 
 def softmax_kernel(q_ref, k_ref, v_ref, live_ref, own_ref, out_ref, own_w_ref, w_scr):
-    rows_per_req = q_ref.shape[0] // live_ref.shape[0]
+    rows = q_ref.shape[1]
+    requests = live_ref.shape[0]
+    per_req = rows // requests
     scores = lax.dot_general(
-        q_ref[...], k_ref[...], (((1,), (1,)), ((), ())), preferred_element_type=jnp.float32
+        q_ref[0], k_ref[...], (((1,), (1,)), ((), ())), preferred_element_type=jnp.float32
     ) * HD ** (-0.5)
-    for r in range(live_ref.shape[0]):
-        rows = slice(r * rows_per_req, (r + 1) * rows_per_req)
-        part = scores[rows, :]
+    for r in range(requests):
+        part_rows = slice(r * per_req, (r + 1) * per_req)
+        part = scores[part_rows, :]
         live = live_ref[r : r + 1, :] != 0
-        own = own_ref[rows, :]
+        own = own_ref[0, part_rows, :]
         top = jnp.maximum(jnp.max(jnp.where(live, part, -1e30), axis=1, keepdims=True), own)
         exp_terms = jnp.where(live, jnp.exp(part - top), 0.0)
         own_exp = jnp.exp(own - top)
         total = jnp.sum(exp_terms, axis=1, keepdims=True) + own_exp
-        w_scr[rows, :] = (exp_terms / total).astype(jnp.bfloat16)
-        own_w_ref[rows, :] = (own_exp / total).astype(jnp.bfloat16).astype(jnp.float32)
-    out_ref[...] = jnp.dot(w_scr[...], v_ref[...], preferred_element_type=jnp.float32)
+        w_scr[part_rows, :] = (exp_terms / total).astype(jnp.bfloat16)
+        own_w_ref[0, part_rows, :] = (own_exp / total).astype(jnp.bfloat16).astype(jnp.float32)
+    out_ref[0] = jnp.dot(w_scr[...], v_ref[...], preferred_element_type=jnp.float32)
 
 
 def attend_pool(queries, new_key, new_value, key_pool, value_pool, lengths, page_table):
@@ -49,34 +51,43 @@
     key_rows = key_pool.reshape(pool_len, kv_width)
     value_rows = value_pool.reshape(pool_len, kv_width)
     grouped = queries.reshape(row_count, groups, per_group, HD)
-    group_eye = jnp.eye(groups, dtype=queries.dtype)
-    spread = (grouped[:, :, :, None, :] * group_eye[None, :, None, :, None]).reshape(
-        row_count * groups * per_group, kv_width
-    )
     own_score = jnp.einsum(
-        "rgqd,rgd->rgq",
+        "rgqd,rgd->grq",
         grouped,
         new_key.reshape(row_count, groups, HD),
         preferred_element_type=jnp.float32,
     ) * HD ** (-0.5)
-    n_rows = row_count * groups * per_group
-    vmem = pl.BlockSpec(memory_space=pltpu.VMEM)
-    flat, own_w = pl.pallas_call(
+    by_group = grouped.transpose(1, 0, 2, 3).reshape(groups, row_count * per_group, HD)
+    n_rows = row_count * per_group
+    per_step = pl.BlockSpec((1, n_rows, HD), lambda g: (g, 0, 0))
+    per_step_col = pl.BlockSpec((1, n_rows, 1), lambda g: (g, 0, 0))
+    lane_slice = pl.BlockSpec((pool_len, HD), lambda g: (0, g))
+    summed, own_w = pl.pallas_call(
         softmax_kernel,
+        grid=(groups,),
         out_shape=(
-            jax.ShapeDtypeStruct((n_rows, kv_width), jnp.float32),
-            jax.ShapeDtypeStruct((n_rows, 1), jnp.float32),
+            jax.ShapeDtypeStruct((groups, n_rows, HD), jnp.float32),
+            jax.ShapeDtypeStruct((groups, n_rows, 1), jnp.float32),
         ),
-        in_specs=[vmem] * 5,
-        out_specs=(vmem, vmem),
+        in_specs=[
+            per_step,
+            lane_slice,
+            lane_slice,
+            pl.BlockSpec((row_count, pool_len), lambda g: (0, 0)),
+            per_step_col,
+        ],
+        out_specs=(per_step, per_step_col),
         scratch_shapes=[pltpu.VMEM((n_rows, pool_len), jnp.bfloat16)],
         interpret=INTERPRET,
-    )(spread, key_rows, value_rows, live_mask.astype(jnp.int32), own_score.reshape(n_rows, 1))
-    every = flat.reshape(row_count, groups, per_group, groups, HD)
-    own_weight = own_w.reshape(row_count, groups, per_group)
-    summed = jnp.sum(
-        every * group_eye.astype(jnp.float32)[None, :, None, :, None], axis=3
+    )(
+        by_group,
+        key_rows,
+        value_rows,
+        live_mask.astype(jnp.int32),
+        own_score.reshape(groups, row_count * per_group, 1),
     )
+    summed = summed.reshape(groups, row_count, per_group, HD).transpose(1, 0, 2, 3)
+    own_weight = own_w.reshape(groups, row_count, per_group).transpose(1, 0, 2)
     summed = summed + own_weight[..., None] * new_value.reshape(
         row_count, groups, 1, HD
     ).astype(jnp.float32)

time: 232 us -> 232 us (level)
  no operation moved by 1% of the time
where the time goes in v6:
time: 232 us; the launch traced here: 231 us
  blocking collectives  125 us (54%)
  waiting for transfers between devices  57.1 us (25%)
  starting transfers between devices  12.4 us (5%)
  matrix products  11.3 us (5%)
  Pallas kernels  10.2 us (4%)
  other arithmetic  9.2 us (4%)
  local copies, waits for them, and re-layouts  6.2 us (3%)
    all_to_all x1, blocking collectives, gather_rows(): gathered = lax.all_to_all(copies, 'req', 0, 0, tiled=True)  66.3 us
    all_to_all x1, blocking collectives, body(): gathered = lax.all_to_all(pieces, 'req', 0, 0, tiled=True)  58.2 us
    all_to_all x1, waiting for transfers between devices, gather_rows(): gathered = lax.all_to_all(copies, 'req', 0, 0, tiled=True)  50.1 us
    all_to_all x1, starting transfers between devices, gather_rows(): gathered = lax.all_to_all(copies, 'req', 0, 0, tiled=True)  11.9 us
    pallas_call x1, Pallas kernels, attend_pool(): pl.pallas_call(softmax_kernel, grid=(groups,), out_shape=(jax.ShapeDtypeS...  10.2 us
  transfers between devices with their start and end apart: 4, of which 4 were waited for; matrix products, arithmetic and copies ran while one was open for 0% of the time, Pallas kernels for 0%

profile of v6, /device:TPU:0, one launch (start us, length us, event | category | flops | bytes accessed | tf_op | source)
XLA Modules:
  0.0 231.2 jit_solution(7638418236803360439)
XLA Ops:
  0.0 0.7 broadcast_compare_fusion
  0.7 0.9 fusion.10
  1.6 0.9 select_reduce_fusion
  2.6 1.5 copy.40
  4.1 1.0 fusion.17
  5.1 0.7 bitcast_convert_fusion
  6.2 0.7 reshape.101.own_ref
  7.3 1.4 fusion.12.live_ref
  8.7 10.2 %shard_map.118 = (f32[4,64,128]{2,1,0:T(8,128)}, f32[4,64,1]{2,1,0:T(8,128)}) custom-call(bf16[4,64,128]{2,1,0:T(8,128)(2,1)} %bitcast.57, bf16[5888,512]{1,0:T(8,128)(2,1)} %bitcast.52, bf16[5888,512]{1,0:T(8,128)(2,1)} %bitcast.53, s32[8,5888]{1,0:T(8,128)} %fusion.12.live_ref, f32[4,64,1]{2,1,0:T(8,128)} %reshape.101.own_ref), custom_call_target="tpu_custom_call" | custom-call | tf_op jit(solution)/shard_map/pallas_call | solution.py:65
  18.9 1.0 reduce
  20.0 1.0 fusion.16
  21.1 2.5 %broadcast_in_dim.18 = bf16[64,8,4096]{2,1,0:T(8,128)(2,1)} broadcast(bf16[8,4096]{1,0:T(8,128)(2,1)S(1)} %bitcast.58), dimensions={1,2} | broadcast | bytes 4259840 | tf_op jit(solution)/shard_map/broadcast_in_dim | solution.py:98
  23.6 11.9 %all-to-all-start = ((bf16[64,8,4096]{2,1,0:T(8,128)(2,1)}), bf16[64,8,4096]{2,1,0:T(8,128)(2,1)}, u32[]{:S(2)}, u32[]{:S(2)}) async-start(bf16[64,8,4096]{2,1,0:T(8,128)(2,1)} %broadcast_in_dim.18), calls=%async_computation | async-start | bytes 8388608 | tf_op jit(solution)/shard_map/all_to_all | solution.py:99
  35.7 1.9 collective-permute-done
  37.6 50.1 %all-to-all-done = bf16[64,8,4096]{2,1,0:T(8,128)(2,1)} async-done(((bf16[64,8,4096]{2,1,0:T(8,128)(2,1)}), bf16[64,8,4096]{2,1,0:T(8,128)(2,1)}, u32[]{:S(2)}, u32[]{:S(2)}) %all-to-all-start) | async-done | bytes 4194336 | tf_op jit(solution)/shard_map/all_to_all | solution.py:99
  87.7 3.7 %fusion = f32[512,128]{0,1:T(8,128)S(1)} fusion(bf16[64,8,4096]{2,1,0:T(8,128)(2,1)} %all-to-all-done, bf16[4096,64]{0,1:T(8,128)(2,1)S(1)} %collective-permute-done, bf16[4096,64]{0,1:T(8,128)(2,1)S(1)} %get-tuple-element.9), kind=kOutput, calls=%fused_computation.1 | convolution fusion | flops 538968064 | bytes 5505024 | tf_op jit(solution)/shard_map/dot_general | solution.py:131
  91.6 1.3 collective-permute-done.1
  93.5 66.3 %all_to_all.15 = bf16[64,64,512]{2,1,0:T(8,128)(2,1)S(1)} all-to-all(bf16[64,64,512]{2,1,0:T(8,128)(2,1)S(1)} %broadcast_in_dim.19), channel_id=1, replica_groups=mesh['head'=2,'req'=64] {'req'}, dimensions={0} | all-to-all | bytes 8388608 | tf_op jit(solution)/shard_map/all_to_all | solution.py:99
  159.8 2.0 fusion.23
  161.8 2.0 fusion.24
  164.3 3.8 %collective-permute-done.2 = f32[512,896]{0,1:T(8,128)S(1)} collective-permute-done((f32[512,896]{0,1:T(8,128)S(1)}, f32[512,896]{0,1:T(8,128)S(1)}, u32[]{:S(2)}, u32[]{:S(2)}) %collective-permute-start.2) | collective-permute-done | bytes 1835040 | tf_op jit(solution)/shard_map/ppermute | solution.py:143
  168.5 2.5 %fusion.6 = f32[512,4096]{0,1:S(1)} fusion(bf16[448,4096]{1,0:T(8,128)(2,1)S(1)} %copy-done.6, f32[512,896]{0,1:T(8,128)S(1)} %fusion.22), kind=kOutput, calls=%fused_computation.10 | convolution fusion | flops 1880424448 | bytes 13893632
  171.7 58.2 %all_to_all.16 = bf16[64,512,64]{1,2,0:T(8,128)(2,1)S(1)} all-to-all(bf16[64,512,64]{1,2,0:T(8,128)(2,1)S(1)} %convert_bitcast_fusion), channel_id=1, replica_groups=mesh['head'=2,'req'=64] {'req'}, dimensions={0} | all-to-all | bytes 8388608 | tf_op jit(solution)/shard_map/all_to_all | solution.py:152
  230.6 0.6 add_convert_fusion
  (37 shorter events, 3.8 us)
Async XLA Ops:
  0.0 4.1 %copy-start = (bf16[8,512]{1,0:T(8,128)(2,1)S(1)}, bf16[8,512]{1,0:T(8,128)(2,1)}, u32[]{:S(2)}) copy-start(bf16[8,512]{1,0:T(8,128)(2,1)} %param.13) | copy-start | bytes 24580
  23.6 11.9 %copy-start.2 = (bf16[8192,64]{0,1:T(8,128)(2,1)S(1)}, bf16[8192,64]{0,1:T(8,128)(2,1)}, u32[]{:S(2)}) copy-start(bf16[8192,64]{0,1:T(8,128)(2,1)} %param.20) | copy-start | bytes 3145732
  23.6 64.2 %all-to-all-start = ((bf16[64,8,4096]{2,1,0:T(8,128)(2,1)}), bf16[64,8,4096]{2,1,0:T(8,128)(2,1)}, u32[]{:S(2)}, u32[]{:S(2)}) async-start(bf16[64,8,4096]{2,1,0:T(8,128)(2,1)} %broadcast_in_dim.18), calls=%async_computation | async-start | bytes 8388608 | tf_op jit(solution)/shard_map/all_to_all | solution.py:99
  35.6 57.3 %copy-start.3 = (bf16[512,64]{0,1:T(8,128)(2,1)S(1)}, bf16[512,64]{0,1:T(8,128)(2,1)}, u32[]{:S(2)}) copy-start(bf16[512,64]{0,1:T(8,128)(2,1)} %param.19) | copy-start | bytes 196612
  35.6 2.0 collective-permute-start
  91.5 1.4 collective-permute-start.1
  93.4 66.3 %copy-start.4 = (bf16[4096,448]{0,1:T(8,128)(2,1)S(1)}, bf16[4096,448]{0,1:T(8,128)(2,1)}, u32[]{:S(2)}) copy-start(bf16[4096,448]{0,1:T(8,128)(2,1)} %param.21) | copy-start | bytes 11010052
  159.8 2.1 copy-start.5
  164.0 4.5 %copy-start.6 = (bf16[448,4096]{1,0:T(8,128)(2,1)S(1)}, bf16[448,4096]{1,0:T(8,128)(2,1)}, u32[]{:S(2)}) copy-start(bf16[448,4096]{1,0:T(8,128)(2,1)} %param.23) | copy-start | bytes 11010052
  164.1 4.0 %collective-permute-start.2 = (f32[512,896]{0,1:T(8,128)S(1)}, f32[512,896]{0,1:T(8,128)S(1)}, u32[]{:S(2)}, u32[]{:S(2)}) collective-permute-start(f32[512,896]{0,1:T(8,128)S(1)} %pad_maximum_fusion), channel_id=1, source_target_pairs={{0,64},{64,0},{1,65},{65,1},{2,66},{66,2},{3,67},{67,3},{4,68},{68... | collective-permute-start | bytes 5505032 | tf_op jit(solution)/shard_map/ppermute | solution.py:143
  171.7 59.5 %copy-start.1 = (bf16[8,512]{1,0:T(8,128)(2,1)S(1)}, bf16[8,512]{1,0:T(8,128)(2,1)}, u32[]{:S(2)}) copy-start(bf16[8,512]{1,0:T(8,128)(2,1)} %param.13) | copy-start | bytes 24580

commit v7 on v6

--- a/solution.py
+++ b/solution.py
@@ -9,25 +9,31 @@
 INTERPRET = False
 
 
-def softmax_kernel(q_ref, k_ref, v_ref, live_ref, own_ref, out_ref, own_w_ref, w_scr):
+def softmax_kernel(q_ref, k_ref, v_ref, live_ref, nk_ref, nv_ref, out_ref, w_scr, own_scr):
     rows = q_ref.shape[1]
     requests = live_ref.shape[0]
     per_req = rows // requests
+    q = q_ref[0]
     scores = lax.dot_general(
-        q_ref[0], k_ref[...], (((1,), (1,)), ((), ())), preferred_element_type=jnp.float32
+        q, k_ref[...], (((1,), (1,)), ((), ())), preferred_element_type=jnp.float32
+    ) * HD ** (-0.5)
+    own_all = lax.dot_general(
+        q, nk_ref[...], (((1,), (1,)), ((), ())), preferred_element_type=jnp.float32
     ) * HD ** (-0.5)
     for r in range(requests):
         part_rows = slice(r * per_req, (r + 1) * per_req)
         part = scores[part_rows, :]
         live = live_ref[r : r + 1, :] != 0
-        own = own_ref[0, part_rows, :]
+        own = own_all[part_rows, r : r + 1]
         top = jnp.maximum(jnp.max(jnp.where(live, part, -1e30), axis=1, keepdims=True), own)
         exp_terms = jnp.where(live, jnp.exp(part - top), 0.0)
         own_exp = jnp.exp(own - top)
         total = jnp.sum(exp_terms, axis=1, keepdims=True) + own_exp
         w_scr[part_rows, :] = (exp_terms / total).astype(jnp.bfloat16)
-        own_w_ref[0, part_rows, :] = (own_exp / total).astype(jnp.bfloat16).astype(jnp.float32)
-    out_ref[0] = jnp.dot(w_scr[...], v_ref[...], preferred_element_type=jnp.float32)
+        own_weight = (own_exp / total).astype(jnp.bfloat16).astype(jnp.float32)
+        own_scr[part_rows, :] = own_weight * nv_ref[r : r + 1, :].astype(jnp.float32)
+    summed = jnp.dot(w_scr[...], v_ref[...], preferred_element_type=jnp.float32) + own_scr[...]
+    out_ref[0] = summed.astype(out_ref.dtype)
 
 
 def attend_pool(queries, new_key, new_value, key_pool, value_pool, lengths, page_table):
@@ -51,47 +57,32 @@
     key_rows = key_pool.reshape(pool_len, kv_width)
     value_rows = value_pool.reshape(pool_len, kv_width)
     grouped = queries.reshape(row_count, groups, per_group, HD)
-    own_score = jnp.einsum(
-        "rgqd,rgd->grq",
-        grouped,
-        new_key.reshape(row_count, groups, HD),
-        preferred_element_type=jnp.float32,
-    ) * HD ** (-0.5)
     by_group = grouped.transpose(1, 0, 2, 3).reshape(groups, row_count * per_group, HD)
     n_rows = row_count * per_group
     per_step = pl.BlockSpec((1, n_rows, HD), lambda g: (g, 0, 0))
-    per_step_col = pl.BlockSpec((1, n_rows, 1), lambda g: (g, 0, 0))
     lane_slice = pl.BlockSpec((pool_len, HD), lambda g: (0, g))
-    summed, own_w = pl.pallas_call(
+    new_slice = pl.BlockSpec((row_count, HD), lambda g: (0, g))
+    summed = pl.pallas_call(
         softmax_kernel,
         grid=(groups,),
-        out_shape=(
-            jax.ShapeDtypeStruct((groups, n_rows, HD), jnp.float32),
-            jax.ShapeDtypeStruct((groups, n_rows, 1), jnp.float32),
-        ),
+        out_shape=jax.ShapeDtypeStruct((groups, n_rows, HD), jnp.bfloat16),
         in_specs=[
             per_step,
             lane_slice,
             lane_slice,
             pl.BlockSpec((row_count, pool_len), lambda g: (0, 0)),
-            per_step_col,
+            new_slice,
+            new_slice,
         ],
-        out_specs=(per_step, per_step_col),
-        scratch_shapes=[pltpu.VMEM((n_rows, pool_len), jnp.bfloat16)],
+        out_specs=per_step,
+        scratch_shapes=[
+            pltpu.VMEM((n_rows, pool_len), jnp.bfloat16),
+            pltpu.VMEM((n_rows, HD), jnp.float32),
+        ],
         interpret=INTERPRET,
-    )(
-        by_group,
-        key_rows,
-        value_rows,
-        live_mask.astype(jnp.int32),
-        own_score.reshape(groups, row_count * per_group, 1),
-    )
+    )(by_group, key_rows, value_rows, live_mask.astype(jnp.int32), new_key, new_value)
     summed = summed.reshape(groups, row_count, per_group, HD).transpose(1, 0, 2, 3)
-    own_weight = own_w.reshape(groups, row_count, per_group).transpose(1, 0, 2)
-    summed = summed + own_weight[..., None] * new_value.reshape(
-        row_count, groups, 1, HD
-    ).astype(jnp.float32)
-    return summed.reshape(row_count, -1).astype(jnp.bfloat16)
+    return summed.reshape(row_count, -1)
 
 
 def gather_rows(block, n_req):

time: 232 us -> 228 us (0.983)
  other arithmetic: 9.2 us -> 6.5 us
where the time goes in v7:
time: 228 us; the launch traced here: 227 us
  blocking collectives  125 us (55%)
  waiting for transfers between devices  56.7 us (25%)
  starting transfers between devices  12.4 us (5%)
  matrix products  10.3 us (5%)
  Pallas kernels  10.2 us (4%)
  other arithmetic  6.5 us (3%)
  local copies, waits for them, and re-layouts  6.2 us (3%)
    all_to_all x1, blocking collectives, gather_rows(): gathered = lax.all_to_all(copies, 'req', 0, 0, tiled=True)  66.6 us
    all_to_all x1, blocking collectives, body(): gathered = lax.all_to_all(pieces, 'req', 0, 0, tiled=True)  58.2 us
    all_to_all x1, waiting for transfers between devices, gather_rows(): gathered = lax.all_to_all(copies, 'req', 0, 0, tiled=True)  49.7 us
    all_to_all x1, starting transfers between devices, gather_rows(): gathered = lax.all_to_all(copies, 'req', 0, 0, tiled=True)  11.9 us
    pallas_call x1, Pallas kernels, attend_pool(): pl.pallas_call(softmax_kernel, grid=(groups,), out_shape=jax.ShapeDtypeSt...  10.2 us
  transfers between devices with their start and end apart: 4, of which 4 were waited for; matrix products, arithmetic and copies ran while one was open for 0% of the time, Pallas kernels for 0%

profile of v7, /device:TPU:0, one launch (start us, length us, event | category | flops | bytes accessed | tf_op | source)
XLA Modules:
  0.0 227.3 jit_solution(3133572123442121539)
XLA Ops:
  0.0 0.7 broadcast_compare_fusion
  0.7 0.9 fusion.10
  1.6 0.9 select_reduce_fusion
  2.6 1.5 copy.26
  4.8 1.4 fusion.12.live_ref
  6.2 10.2 %shard_map.118 = bf16[4,64,128]{2,1,0:T(8,128)(2,1)} custom-call(bf16[4,64,128]{2,1,0:T(8,128)(2,1)} %bitcast.42, bf16[5888,512]{1,0:T(8,128)(2,1)} %bitcast.37, bf16[5888,512]{1,0:T(8,128)(2,1)} %bitcast.38, s32[8,5888]{1,0:T(8,128)} %fusion.12.live_ref, bf16[8,512]{1,0:T(8,128)(2,1)} %nk_ref.1, bf16[8,512]{1,0:T(8,128)(2,1)} %nv_ref.1), custom_call_target="tpu_custom_call" | custom-call | tf_op jit(solution)/shard_map/pallas_call | solution.py:65
  16.4 0.9 copy_bitcast_fusion.1
  17.3 2.5 %broadcast_in_dim.21 = bf16[64,8,4096]{2,1,0:T(8,128)(2,1)} broadcast(bf16[8,4096]{1,0:T(8,128)(2,1)S(1)} %bitcast.43), dimensions={1,2} | broadcast | bytes 4259840 | tf_op jit(solution)/shard_map/broadcast_in_dim | solution.py:89
  19.8 11.9 %all-to-all-start = ((bf16[64,8,4096]{2,1,0:T(8,128)(2,1)}), bf16[64,8,4096]{2,1,0:T(8,128)(2,1)}, u32[]{:S(2)}, u32[]{:S(2)}) async-start(bf16[64,8,4096]{2,1,0:T(8,128)(2,1)} %broadcast_in_dim.21), calls=%async_computation | async-start | bytes 8388608 | tf_op jit(solution)/shard_map/all_to_all | solution.py:90
  32.0 1.9 collective-permute-done
  33.9 49.7 %all-to-all-done = bf16[64,8,4096]{2,1,0:T(8,128)(2,1)} async-done(((bf16[64,8,4096]{2,1,0:T(8,128)(2,1)}), bf16[64,8,4096]{2,1,0:T(8,128)(2,1)}, u32[]{:S(2)}, u32[]{:S(2)}) %all-to-all-start) | async-done | bytes 4194336 | tf_op jit(solution)/shard_map/all_to_all | solution.py:90
  83.5 3.7 %fusion = f32[512,128]{0,1:T(8,128)S(1)} fusion(bf16[64,8,4096]{2,1,0:T(8,128)(2,1)} %all-to-all-done, bf16[4096,64]{0,1:T(8,128)(2,1)S(1)} %collective-permute-done, bf16[4096,64]{0,1:T(8,128)(2,1)S(1)} %get-tuple-element.5), kind=kOutput, calls=%fused_computation.1 | convolution fusion | flops 538968064 | bytes 5505024 | tf_op jit(solution)/shard_map/dot_general | solution.py:122
  87.4 1.3 collective-permute-done.1
  88.7 0.5 broadcast_in_dim.36
  89.3 66.6 %all_to_all.15 = bf16[64,64,512]{2,1,0:T(8,128)(2,1)S(1)} all-to-all(bf16[64,64,512]{2,1,0:T(8,128)(2,1)S(1)} %broadcast_in_dim.36), channel_id=1, replica_groups=mesh['head'=2,'req'=64] {'req'}, dimensions={0} | all-to-all | bytes 8388608 | tf_op jit(solution)/shard_map/all_to_all | solution.py:90
  155.8 2.0 fusion.18
  157.9 2.1 fusion.19
  160.4 3.8 %collective-permute-done.2 = f32[512,896]{0,1:T(8,128)S(1)} collective-permute-done((f32[512,896]{0,1:T(8,128)S(1)}, f32[512,896]{0,1:T(8,128)S(1)}, u32[]{:S(2)}, u32[]{:S(2)}) %collective-permute-start.2) | collective-permute-done | bytes 1835040 | tf_op jit(solution)/shard_map/ppermute | solution.py:134
  164.2 0.4 fusion.17
  164.6 2.5 %fusion.6 = f32[512,4096]{0,1:S(1)} fusion(bf16[448,4096]{1,0:T(8,128)(2,1)S(1)} %copy-done.4, f32[512,896]{0,1:T(8,128)S(1)} %fusion.17), kind=kOutput, calls=%fused_computation.10 | convolution fusion | flops 1880424448 | bytes 13893632
  167.1 0.6 convert_bitcast_fusion
  167.8 58.2 %all_to_all.16 = bf16[64,512,64]{1,2,0:T(8,128)(2,1)S(1)} all-to-all(bf16[64,512,64]{1,2,0:T(8,128)(2,1)S(1)} %convert_bitcast_fusion), channel_id=1, replica_groups=mesh['head'=2,'req'=64] {'req'}, dimensions={0} | all-to-all | bytes 8388608 | tf_op jit(solution)/shard_map/all_to_all | solution.py:143
  226.0 0.7 convert_reduce_fusion
  226.6 0.7 add_convert_fusion
  (25 shorter events, 1.5 us)
Async XLA Ops:
  19.8 11.9 %copy-start = (bf16[8192,64]{0,1:T(8,128)(2,1)S(1)}, bf16[8192,64]{0,1:T(8,128)(2,1)}, u32[]{:S(2)}) copy-start(bf16[8192,64]{0,1:T(8,128)(2,1)} %param.20) | copy-start | bytes 3145732
  19.8 63.7 %all-to-all-start = ((bf16[64,8,4096]{2,1,0:T(8,128)(2,1)}), bf16[64,8,4096]{2,1,0:T(8,128)(2,1)}, u32[]{:S(2)}, u32[]{:S(2)}) async-start(bf16[64,8,4096]{2,1,0:T(8,128)(2,1)} %broadcast_in_dim.21), calls=%async_computation | async-start | bytes 8388608 | tf_op jit(solution)/shard_map/all_to_all | solution.py:90
  31.9 56.8 %copy-start.1 = (bf16[512,64]{0,1:T(8,128)(2,1)S(1)}, bf16[512,64]{0,1:T(8,128)(2,1)}, u32[]{:S(2)}) copy-start(bf16[512,64]{0,1:T(8,128)(2,1)} %param.19) | copy-start | bytes 196612
  31.9 2.0 collective-permute-start
  87.3 1.4 collective-permute-start.1
  89.2 66.6 %copy-start.2 = (bf16[4096,448]{0,1:T(8,128)(2,1)S(1)}, bf16[4096,448]{0,1:T(8,128)(2,1)}, u32[]{:S(2)}) copy-start(bf16[4096,448]{0,1:T(8,128)(2,1)} %param.21) | copy-start | bytes 11010052
  155.8 2.1 copy-start.3
  160.1 4.5 %copy-start.4 = (bf16[448,4096]{1,0:T(8,128)(2,1)S(1)}, bf16[448,4096]{1,0:T(8,128)(2,1)}, u32[]{:S(2)}) copy-start(bf16[448,4096]{1,0:T(8,128)(2,1)} %param.23) | copy-start | bytes 11010052
  160.1 4.0 %collective-permute-start.2 = (f32[512,896]{0,1:T(8,128)S(1)}, f32[512,896]{0,1:T(8,128)S(1)}, u32[]{:S(2)}, u32[]{:S(2)}) collective-permute-start(f32[512,896]{0,1:T(8,128)S(1)} %pad_maximum_fusion), channel_id=1, source_target_pairs={{0,64},{64,0},{1,65},{65,1},{2,66},{66,2},{3,67},{67,3},{4,68},{68... | collective-permute-start | bytes 5505032 | tf_op jit(solution)/shard_map/ppermute | solution.py:134

commit v8 on v7

--- a/solution.py
+++ b/solution.py
@@ -9,11 +9,14 @@
 INTERPRET = False
 
 
-def softmax_kernel(q_ref, k_ref, v_ref, live_ref, nk_ref, nv_ref, out_ref, w_scr, own_scr):
-    rows = q_ref.shape[1]
+def softmax_kernel(q_ref, k_ref, v_ref, live_ref, nk_ref, nv_ref, out_ref, q_scr, w_scr, own_scr):
+    rows = q_scr.shape[0]
     requests = live_ref.shape[0]
     per_req = rows // requests
-    q = q_ref[0]
+    for r in range(requests):
+        for h in range(per_req):
+            q_scr[r * per_req + h : r * per_req + h + 1, :] = q_ref[r : r + 1, h * HD : (h + 1) * HD]
+    q = q_scr[...]
     scores = lax.dot_general(
         q, k_ref[...], (((1,), (1,)), ((), ())), preferred_element_type=jnp.float32
     ) * HD ** (-0.5)
@@ -32,8 +35,10 @@
         w_scr[part_rows, :] = (exp_terms / total).astype(jnp.bfloat16)
         own_weight = (own_exp / total).astype(jnp.bfloat16).astype(jnp.float32)
         own_scr[part_rows, :] = own_weight * nv_ref[r : r + 1, :].astype(jnp.float32)
-    summed = jnp.dot(w_scr[...], v_ref[...], preferred_element_type=jnp.float32) + own_scr[...]
-    out_ref[0] = summed.astype(out_ref.dtype)
+    own_scr[...] = jnp.dot(w_scr[...], v_ref[...], preferred_element_type=jnp.float32) + own_scr[...]
+    for r in range(requests):
+        for h in range(per_req):
+            out_ref[r : r + 1, h * HD : (h + 1) * HD] = own_scr[r * per_req + h : r * per_req + h + 1, :]
 
 
 def attend_pool(queries, new_key, new_value, key_pool, value_pool, lengths, page_table):
@@ -56,33 +61,31 @@
 
     key_rows = key_pool.reshape(pool_len, kv_width)
     value_rows = value_pool.reshape(pool_len, kv_width)
-    grouped = queries.reshape(row_count, groups, per_group, HD)
-    by_group = grouped.transpose(1, 0, 2, 3).reshape(groups, row_count * per_group, HD)
     n_rows = row_count * per_group
-    per_step = pl.BlockSpec((1, n_rows, HD), lambda g: (g, 0, 0))
+    group_cols = pl.BlockSpec((row_count, per_group * HD), lambda g: (0, g))
     lane_slice = pl.BlockSpec((pool_len, HD), lambda g: (0, g))
     new_slice = pl.BlockSpec((row_count, HD), lambda g: (0, g))
     summed = pl.pallas_call(
         softmax_kernel,
         grid=(groups,),
-        out_shape=jax.ShapeDtypeStruct((groups, n_rows, HD), jnp.bfloat16),
+        out_shape=jax.ShapeDtypeStruct((row_count, groups * per_group * HD), jnp.float32),
         in_specs=[
-            per_step,
+            group_cols,
             lane_slice,
             lane_slice,
             pl.BlockSpec((row_count, pool_len), lambda g: (0, 0)),
             new_slice,
             new_slice,
         ],
-        out_specs=per_step,
+        out_specs=group_cols,
         scratch_shapes=[
+            pltpu.VMEM((n_rows, HD), queries.dtype),
             pltpu.VMEM((n_rows, pool_len), jnp.bfloat16),
             pltpu.VMEM((n_rows, HD), jnp.float32),
         ],
         interpret=INTERPRET,
-    )(by_group, key_rows, value_rows, live_mask.astype(jnp.int32), new_key, new_value)
-    summed = summed.reshape(groups, row_count, per_group, HD).transpose(1, 0, 2, 3)
-    return summed.reshape(row_count, -1)
+    )(queries, key_rows, value_rows, live_mask.astype(jnp.int32), new_key, new_value)
+    return summed.astype(jnp.bfloat16)
 
 
 def gather_rows(block, n_req):

time: 228 us -> 226 us (level)
  local copies, waits for them, and re-layouts: 6.2 us -> 3.85 us
where the time goes in v8:
time: 226 us
  blocking collectives  124 us (55%)
  waiting for transfers between devices  57 us (25%)
  starting transfers between devices  12.4 us (5%)
  matrix products  10.4 us (5%)
  Pallas kernels  10.3 us (5%)
  other arithmetic  7.41 us (3%)
  local copies, waits for them, and re-layouts  3.85 us (2%)
    all_to_all x1, blocking collectives, gather_rows(): gathered = lax.all_to_all(copies, 'req', 0, 0, tiled=True)  66.2 us
    all_to_all x1, blocking collectives, body(): gathered = lax.all_to_all(pieces, 'req', 0, 0, tiled=True)  58.2 us
    all_to_all x1, waiting for transfers between devices, gather_rows(): gathered = lax.all_to_all(copies, 'req', 0, 0, tiled=True)  50 us
    all_to_all x1, starting transfers between devices, gather_rows(): gathered = lax.all_to_all(copies, 'req', 0, 0, tiled=True)  11.9 us
    pallas_call x1, Pallas kernels, attend_pool(): pl.pallas_call(softmax_kernel, grid=(groups,), out_shape=jax.ShapeDtypeSt...  10.3 us
  transfers between devices with their start and end apart: 4, of which 4 were waited for; matrix products, arithmetic and copies ran while one was open for 0% of the time, Pallas kernels for 0%

profile of v8, /device:TPU:0, one launch (start us, length us, event | category | flops | bytes accessed | tf_op | source)
XLA Modules:
  0.0 225.8 jit_solution(2210968517932660378)
XLA Ops:
  0.0 0.7 broadcast_compare_fusion
  0.7 0.9 fusion.10
  1.6 0.9 select_reduce_fusion
  3.3 1.4 fusion.12.live_ref
  4.7 10.3 %shard_map.118 = f32[8,4096]{1,0:T(8,128)} custom-call(bf16[8,4096]{1,0:T(8,128)(2,1)} %q_ref.1, bf16[5888,512]{1,0:T(8,128)(2,1)} %bitcast.21, bf16[5888,512]{1,0:T(8,128)(2,1)} %bitcast.22, s32[8,5888]{1,0:T(8,128)} %fusion.12.live_ref, bf16[8,512]{1,0:T(8,128)(2,1)} %nk_ref.1, bf16[8,512]{1,0:T(8,128)(2,1)} %nv_ref.1), custom_call_target="tpu_custom_call" | custom-call | tf_op jit(solution)/shard_map/pallas_call | solution.py:68
  15.0 0.9 convert_element_type.32
  16.0 2.5 %broadcast_in_dim.18 = bf16[64,8,4096]{2,1,0:T(8,128)(2,1)} broadcast(bf16[8,4096]{1,0:T(8,128)(2,1)S(1)} %convert_element_type.32), dimensions={1,2} | broadcast | bytes 4259840 | tf_op jit(solution)/shard_map/broadcast_in_dim | solution.py:92
  18.4 11.9 %all-to-all-start = ((bf16[64,8,4096]{2,1,0:T(8,128)(2,1)}), bf16[64,8,4096]{2,1,0:T(8,128)(2,1)}, u32[]{:S(2)}, u32[]{:S(2)}) async-start(bf16[64,8,4096]{2,1,0:T(8,128)(2,1)} %broadcast_in_dim.18), calls=%async_computation | async-start | bytes 8388608 | tf_op jit(solution)/shard_map/all_to_all | solution.py:93
  30.6 1.9 collective-permute-done
  32.5 50.0 %all-to-all-done = bf16[64,8,4096]{2,1,0:T(8,128)(2,1)} async-done(((bf16[64,8,4096]{2,1,0:T(8,128)(2,1)}), bf16[64,8,4096]{2,1,0:T(8,128)(2,1)}, u32[]{:S(2)}, u32[]{:S(2)}) %all-to-all-start) | async-done | bytes 4194336 | tf_op jit(solution)/shard_map/all_to_all | solution.py:93
  82.4 3.7 %fusion = f32[512,128]{0,1:T(8,128)S(1)} fusion(bf16[64,8,4096]{2,1,0:T(8,128)(2,1)} %all-to-all-done, bf16[4096,64]{0,1:T(8,128)(2,1)S(1)} %collective-permute-done, bf16[4096,64]{0,1:T(8,128)(2,1)S(1)} %get-tuple-element.5), kind=kOutput, calls=%fused_computation.1 | convolution fusion | flops 538968064 | bytes 5505024 | tf_op jit(solution)/shard_map/dot_general | solution.py:125
  86.3 1.3 collective-permute-done.1
  87.7 0.5 broadcast_in_dim.19
  88.2 66.2 %all_to_all.15 = bf16[64,64,512]{2,1,0:T(8,128)(2,1)S(1)} all-to-all(bf16[64,64,512]{2,1,0:T(8,128)(2,1)S(1)} %broadcast_in_dim.19), channel_id=1, replica_groups=mesh['head'=2,'req'=64] {'req'}, dimensions={0} | all-to-all | bytes 8388608 | tf_op jit(solution)/shard_map/all_to_all | solution.py:93
  154.4 2.0 fusion.18
  156.5 2.1 fusion.19
  158.7 0.3 collective-permute-start.2
  158.9 3.8 %collective-permute-done.2 = f32[512,896]{0,1:T(8,128)S(1)} collective-permute-done((f32[512,896]{0,1:T(8,128)S(1)}, f32[512,896]{0,1:T(8,128)S(1)}, u32[]{:S(2)}, u32[]{:S(2)}) %collective-permute-start.2) | collective-permute-done | bytes 1835040 | tf_op jit(solution)/shard_map/ppermute | solution.py:137
  162.7 0.4 fusion.17
  163.1 2.5 %fusion.6 = f32[512,4096]{0,1:S(1)} fusion(bf16[448,4096]{1,0:T(8,128)(2,1)S(1)} %copy-done.4, f32[512,896]{0,1:T(8,128)S(1)} %fusion.17), kind=kOutput, calls=%fused_computation.10 | convolution fusion | flops 1880424448 | bytes 13893632
  165.7 0.6 convert_bitcast_fusion
  166.3 58.2 %all_to_all.16 = bf16[64,512,64]{1,2,0:T(8,128)(2,1)S(1)} all-to-all(bf16[64,512,64]{1,2,0:T(8,128)(2,1)S(1)} %convert_bitcast_fusion), channel_id=1, replica_groups=mesh['head'=2,'req'=64] {'req'}, dimensions={0} | all-to-all | bytes 8388608 | tf_op jit(solution)/shard_map/all_to_all | solution.py:146
  224.5 0.7 convert_reduce_fusion
  225.2 0.7 add_convert_fusion
  (23 shorter events, 1.2 us)
Async XLA Ops:
  18.4 11.9 %copy-start = (bf16[8192,64]{0,1:T(8,128)(2,1)S(1)}, bf16[8192,64]{0,1:T(8,128)(2,1)}, u32[]{:S(2)}) copy-start(bf16[8192,64]{0,1:T(8,128)(2,1)} %param.20) | copy-start | bytes 3145732
  18.4 64.0 %all-to-all-start = ((bf16[64,8,4096]{2,1,0:T(8,128)(2,1)}), bf16[64,8,4096]{2,1,0:T(8,128)(2,1)}, u32[]{:S(2)}, u32[]{:S(2)}) async-start(bf16[64,8,4096]{2,1,0:T(8,128)(2,1)} %broadcast_in_dim.18), calls=%async_computation | async-start | bytes 8388608 | tf_op jit(solution)/shard_map/all_to_all | solution.py:93
  30.5 57.1 %copy-start.1 = (bf16[512,64]{0,1:T(8,128)(2,1)S(1)}, bf16[512,64]{0,1:T(8,128)(2,1)}, u32[]{:S(2)}) copy-start(bf16[512,64]{0,1:T(8,128)(2,1)} %param.19) | copy-start | bytes 196612
  30.5 2.0 collective-permute-start
  86.2 1.4 collective-permute-start.1
  88.2 66.2 %copy-start.2 = (bf16[4096,448]{0,1:T(8,128)(2,1)S(1)}, bf16[4096,448]{0,1:T(8,128)(2,1)}, u32[]{:S(2)}) copy-start(bf16[4096,448]{0,1:T(8,128)(2,1)} %param.21) | copy-start | bytes 11010052
  154.4 2.1 copy-start.3
  158.7 4.5 %copy-start.4 = (bf16[448,4096]{1,0:T(8,128)(2,1)S(1)}, bf16[448,4096]{1,0:T(8,128)(2,1)}, u32[]{:S(2)}) copy-start(bf16[448,4096]{1,0:T(8,128)(2,1)} %param.23) | copy-start | bytes 11010052
  158.7 4.0 %collective-permute-start.2 = (f32[512,896]{0,1:T(8,128)S(1)}, f32[512,896]{0,1:T(8,128)S(1)}, u32[]{:S(2)}, u32[]{:S(2)}) collective-permute-start(f32[512,896]{0,1:T(8,128)S(1)} %pad_maximum_fusion), channel_id=1, source_target_pairs={{0,64},{64,0},{1,65},{65,1},{2,66},{66,2},{3,67},{67,3},{4,68},{68... | collective-permute-start | bytes 5505032 | tf_op jit(solution)/shard_map/ppermute | solution.py:137

commit v9 on v8

--- a/solution.py
+++ b/solution.py
@@ -9,7 +9,7 @@
 INTERPRET = False
 
 
-def softmax_kernel(q_ref, k_ref, v_ref, live_ref, nk_ref, nv_ref, out_ref, q_scr, w_scr, own_scr):
+def softmax_kernel(q_ref, k_ref, v_ref, live_ref, nk_ref, nv_ref, out_ref, q_scr, w_scr, own_scr, att_scr):
     rows = q_scr.shape[0]
     requests = live_ref.shape[0]
     per_req = rows // requests
@@ -38,10 +38,11 @@
     own_scr[...] = jnp.dot(w_scr[...], v_ref[...], preferred_element_type=jnp.float32) + own_scr[...]
     for r in range(requests):
         for h in range(per_req):
-            out_ref[r : r + 1, h * HD : (h + 1) * HD] = own_scr[r * per_req + h : r * per_req + h + 1, :]
+            att_scr[r : r + 1, h * HD : (h + 1) * HD] = own_scr[r * per_req + h : r * per_req + h + 1, :]
+    out_ref[...] = jnp.broadcast_to(att_scr[...].astype(out_ref.dtype)[None], out_ref.shape)
 
 
-def attend_pool(queries, new_key, new_value, key_pool, value_pool, lengths, page_table):
+def attend_pool(queries, new_key, new_value, key_pool, value_pool, lengths, page_table, copies):
     row_count = queries.shape[0]
     pool_pages, page_rows, kv_width = key_pool.shape
     groups = kv_width // HD
@@ -68,7 +69,7 @@
     summed = pl.pallas_call(
         softmax_kernel,
         grid=(groups,),
-        out_shape=jax.ShapeDtypeStruct((row_count, groups * per_group * HD), jnp.float32),
+        out_shape=jax.ShapeDtypeStruct((copies, row_count, groups * per_group * HD), jnp.bfloat16),
         in_specs=[
             group_cols,
             lane_slice,
@@ -77,15 +78,16 @@
             new_slice,
             new_slice,
         ],
-        out_specs=group_cols,
+        out_specs=pl.BlockSpec((copies, row_count, per_group * HD), lambda g: (0, 0, g)),
         scratch_shapes=[
             pltpu.VMEM((n_rows, HD), queries.dtype),
             pltpu.VMEM((n_rows, pool_len), jnp.bfloat16),
             pltpu.VMEM((n_rows, HD), jnp.float32),
+            pltpu.VMEM((row_count, per_group * HD), jnp.float32),
         ],
         interpret=INTERPRET,
     )(queries, key_rows, value_rows, live_mask.astype(jnp.int32), new_key, new_value)
-    return summed.astype(jnp.bfloat16)
+    return summed
 
 
 def gather_rows(block, n_req):
@@ -118,10 +120,12 @@
     lent_rows = lax.ppermute(partner_rows, "head", swap)
     own_rows = lax.dynamic_slice_in_dim(out_weight, head * half, half, axis=0)
 
-    attention = attend_pool(
-        queries, new_key, new_value, key_cache, value_cache, lengths, page_table
+    attention_copies = attend_pool(
+        queries, new_key, new_value, key_cache, value_cache, lengths, page_table, n_req
     )
-    features = gather_rows(attention, n_req)
+    features = lax.all_to_all(attention_copies, "req", 0, 0, tiled=True).reshape(
+        -1, attention_copies.shape[2]
+    )
     both = jnp.dot(
         features,
         jnp.concatenate([own_rows, lent_rows], axis=1),

time: 226 us -> 224 us (level)
  local copies, waits for them, and re-layouts: 3.85 us -> 1.37 us
    broadcast_in_dim x2 -> x1, local copies, waits for them, and re-layouts: 2.97 us -> 0.49 us  [gather_rows(): copies = jnp.broadcast_to(block[None], (n_req,) + block.shape)]
where the time goes in v9:
time: 224 us
  blocking collectives  125 us (56%)
  waiting for transfers between devices  57.1 us (25%)
  starting transfers between devices  12.4 us (6%)
  Pallas kernels  11.5 us (5%)
  matrix products  10.3 us (5%)
  other arithmetic  6.46 us (3%)
    all_to_all x1, blocking collectives, gather_rows(): gathered = lax.all_to_all(copies, 'req', 0, 0, tiled=True)  66.3 us
    all_to_all x1, blocking collectives, body(): gathered = lax.all_to_all(pieces, 'req', 0, 0, tiled=True)  58.2 us
    all_to_all x1, waiting for transfers between devices, body(): lax.all_to_all(attention_copies, 'req', 0, 0, tiled=True)  50.1 us
    all_to_all x1, starting transfers between devices, body(): lax.all_to_all(attention_copies, 'req', 0, 0, tiled=True)  11.9 us
    pallas_call x1, Pallas kernels, attend_pool(): pl.pallas_call(softmax_kernel, grid=(groups,), out_shape=jax.ShapeDtypeSt...  11.5 us
  transfers between devices with their start and end apart: 4, of which 4 were waited for; matrix products, arithmetic and copies ran while one was open for 0% of the time, Pallas kernels for 0%

profile of v9, /device:TPU:0, one launch (start us, length us, event | category | flops | bytes accessed | tf_op | source)
XLA Modules:
  0.0 223.8 jit_solution(17799210730275222602)
XLA Ops:
  0.0 0.7 broadcast_compare_fusion
  0.7 0.9 fusion.10
  1.6 0.9 select_reduce_fusion
  2.6 0.2 and.22
  2.8 0.2 and.23
  3.3 1.4 fusion.12.live_ref
  4.7 11.5 %shard_map.118 = bf16[64,8,4096]{2,1,0:T(8,128)(2,1)} custom-call(bf16[8,4096]{1,0:T(8,128)(2,1)} %q_ref.1, bf16[5888,512]{1,0:T(8,128)(2,1)} %bitcast.21, bf16[5888,512]{1,0:T(8,128)(2,1)} %bitcast.22, s32[8,5888]{1,0:T(8,128)} %fusion.12.live_ref, bf16[8,512]{1,0:T(8,128)(2,1)} %nk_ref.1, bf16[8,512]{1,0:T(8,128)(2,1)} %nv_ref.1), custom_call_target="tpu_custom_call" | custom-call | tf_op jit(solution)/shard_map/pallas_call | solution.py:69
  16.2 11.9 %all-to-all-start = ((bf16[64,8,4096]{2,1,0:T(8,128)(2,1)}), bf16[64,8,4096]{2,1,0:T(8,128)(2,1)}, u32[]{:S(2)}, u32[]{:S(2)}) async-start(bf16[64,8,4096]{2,1,0:T(8,128)(2,1)} %shard_map.118), calls=%async_computation | async-start | bytes 8388608 | tf_op jit(solution)/shard_map/all_to_all | solution.py:126
  28.4 1.9 collective-permute-done
  30.3 50.1 %all-to-all-done = bf16[64,8,4096]{2,1,0:T(8,128)(2,1)} async-done(((bf16[64,8,4096]{2,1,0:T(8,128)(2,1)}), bf16[64,8,4096]{2,1,0:T(8,128)(2,1)}, u32[]{:S(2)}, u32[]{:S(2)}) %all-to-all-start) | async-done | bytes 4194336 | tf_op jit(solution)/shard_map/all_to_all | solution.py:126
  80.4 3.7 %fusion = f32[512,128]{0,1:T(8,128)S(1)} fusion(bf16[64,8,4096]{2,1,0:T(8,128)(2,1)} %all-to-all-done, bf16[4096,64]{0,1:T(8,128)(2,1)S(1)} %collective-permute-done, bf16[4096,64]{0,1:T(8,128)(2,1)S(1)} %get-tuple-element.5), kind=kOutput, calls=%fused_computation.1 | convolution fusion | flops 538968064 | bytes 5505024 | tf_op jit(solution)/shard_map/dot_general | solution.py:129
  84.2 1.3 collective-permute-done.1
  85.6 0.5 broadcast_in_dim.16
  86.1 66.3 %all_to_all.15 = bf16[64,64,512]{2,1,0:T(8,128)(2,1)S(1)} all-to-all(bf16[64,64,512]{2,1,0:T(8,128)(2,1)S(1)} %broadcast_in_dim.16), channel_id=1, replica_groups=mesh['head'=2,'req'=64] {'req'}, dimensions={0} | all-to-all | bytes 8388608 | tf_op jit(solution)/shard_map/all_to_all | solution.py:95
  152.4 2.0 fusion.18
  154.5 2.0 fusion.19
  156.7 0.3 collective-permute-start.2
  157.0 3.8 %collective-permute-done.2 = f32[512,896]{0,1:T(8,128)S(1)} collective-permute-done((f32[512,896]{0,1:T(8,128)S(1)}, f32[512,896]{0,1:T(8,128)S(1)}, u32[]{:S(2)}, u32[]{:S(2)}) %collective-permute-start.2) | collective-permute-done | bytes 1835040 | tf_op jit(solution)/shard_map/ppermute | solution.py:141
  160.7 0.4 fusion.17
  161.2 2.5 %fusion.6 = f32[512,4096]{0,1:S(1)} fusion(bf16[448,4096]{1,0:T(8,128)(2,1)S(1)} %copy-done.4, f32[512,896]{0,1:T(8,128)S(1)} %fusion.17), kind=kOutput, calls=%fused_computation.10 | convolution fusion | flops 1880424448 | bytes 13893632
  163.7 0.6 convert_bitcast_fusion
  164.3 58.2 %all_to_all.16 = bf16[64,512,64]{1,2,0:T(8,128)(2,1)S(1)} all-to-all(bf16[64,512,64]{1,2,0:T(8,128)(2,1)S(1)} %convert_bitcast_fusion), channel_id=1, replica_groups=mesh['head'=2,'req'=64] {'req'}, dimensions={0} | all-to-all | bytes 8388608 | tf_op jit(solution)/shard_map/all_to_all | solution.py:150
  222.5 0.6 convert_reduce_fusion
  223.2 0.6 add_convert_fusion
  (21 shorter events, 0.9 us)
Async XLA Ops:
  16.2 11.9 %copy-start = (bf16[8192,64]{0,1:T(8,128)(2,1)S(1)}, bf16[8192,64]{0,1:T(8,128)(2,1)}, u32[]{:S(2)}) copy-start(bf16[8192,64]{0,1:T(8,128)(2,1)} %param.20) | copy-start | bytes 3145732
  16.2 64.2 %all-to-all-start = ((bf16[64,8,4096]{2,1,0:T(8,128)(2,1)}), bf16[64,8,4096]{2,1,0:T(8,128)(2,1)}, u32[]{:S(2)}, u32[]{:S(2)}) async-start(bf16[64,8,4096]{2,1,0:T(8,128)(2,1)} %shard_map.118), calls=%async_computation | async-start | bytes 8388608 | tf_op jit(solution)/shard_map/all_to_all | solution.py:126
  28.3 57.3 %copy-start.1 = (bf16[512,64]{0,1:T(8,128)(2,1)S(1)}, bf16[512,64]{0,1:T(8,128)(2,1)}, u32[]{:S(2)}) copy-start(bf16[512,64]{0,1:T(8,128)(2,1)} %param.19) | copy-start | bytes 196612
  28.3 2.0 collective-permute-start
  84.1 1.4 collective-permute-start.1
  86.1 66.3 %copy-start.2 = (bf16[4096,448]{0,1:T(8,128)(2,1)S(1)}, bf16[4096,448]{0,1:T(8,128)(2,1)}, u32[]{:S(2)}) copy-start(bf16[4096,448]{0,1:T(8,128)(2,1)} %param.21) | copy-start | bytes 11010052
  152.4 2.1 copy-start.3
  156.7 4.5 %copy-start.4 = (bf16[448,4096]{1,0:T(8,128)(2,1)S(1)}, bf16[448,4096]{1,0:T(8,128)(2,1)}, u32[]{:S(2)}) copy-start(bf16[448,4096]{1,0:T(8,128)(2,1)} %param.23) | copy-start | bytes 11010052
  156.7 4.0 %collective-permute-start.2 = (f32[512,896]{0,1:T(8,128)S(1)}, f32[512,896]{0,1:T(8,128)S(1)}, u32[]{:S(2)}, u32[]{:S(2)}) collective-permute-start(f32[512,896]{0,1:T(8,128)S(1)} %pad_maximum_fusion), channel_id=1, source_target_pairs={{0,64},{64,0},{1,65},{65,1},{2,66},{66,2},{3,67},{67,3},{4,68},{68... | collective-permute-start | bytes 5505032 | tf_op jit(solution)/shard_map/ppermute | solution.py:141

commit v10 on v9

--- a/solution.py
+++ b/solution.py
@@ -50,15 +50,11 @@
     pages_max = page_table.shape[1]
     pool_len = pool_pages * page_rows
 
-    slot_start = lax.broadcasted_iota(jnp.int32, (row_count, pages_max), 1) * page_rows
-    slot_live = slot_start < lengths[:, None]
-    match = (page_table[:, :, None] == lax.broadcasted_iota(jnp.int32, (1, 1, pool_pages), 2)) & slot_live[
-        :, :, None
-    ]
-    owned = jnp.any(match, axis=1)
-    base = jnp.sum(jnp.where(match, slot_start[:, :, None], 0), axis=1)
-    position = base[:, :, None] + lax.broadcasted_iota(jnp.int32, (1, 1, page_rows), 2)
-    live_mask = (owned[:, :, None] & (position < lengths[:, None, None])).reshape(row_count, pool_len)
+    slot_ids = lax.broadcasted_iota(jnp.int32, (row_count, pages_max, pool_pages), 1)
+    named = page_table[:, :, None] == lax.broadcasted_iota(jnp.int32, (1, 1, pool_pages), 2)
+    slot_of = jnp.min(jnp.where(named, slot_ids, pages_max), axis=1)
+    position = slot_of[:, :, None] * page_rows + lax.broadcasted_iota(jnp.int32, (1, 1, page_rows), 2)
+    live_mask = (position < lengths[:, None, None]).reshape(row_count, pool_len)
 
     key_rows = key_pool.reshape(pool_len, kv_width)
     value_rows = value_pool.reshape(pool_len, kv_width)

time: 224 us -> 222 us (level)
  no operation moved by 1% of the time
where the time goes in v10:
time: 222 us
  blocking collectives  124 us (56%)
  waiting for transfers between devices  57.1 us (26%)
  starting transfers between devices  12.4 us (6%)
  Pallas kernels  11.5 us (5%)
  matrix products  10.3 us (5%)
  other arithmetic  4.74 us (2%)
    all_to_all x1, blocking collectives, gather_rows(): gathered = lax.all_to_all(copies, 'req', 0, 0, tiled=True)  66.3 us
    all_to_all x1, blocking collectives, body(): gathered = lax.all_to_all(pieces, 'req', 0, 0, tiled=True)  58.2 us
    all_to_all x1, waiting for transfers between devices, body(): lax.all_to_all(attention_copies, 'req', 0, 0, tiled=True)  50.1 us
    all_to_all x1, starting transfers between devices, body(): lax.all_to_all(attention_copies, 'req', 0, 0, tiled=True)  11.9 us
    pallas_call x1, Pallas kernels, attend_pool(): pl.pallas_call(softmax_kernel, grid=(groups,), out_shape=jax.ShapeDtypeSt...  11.5 us
  transfers between devices with their start and end apart: 4, of which 4 were waited for; matrix products, arithmetic and copies ran while one was open for 0% of the time, Pallas kernels for 0%

profile of v10, /device:TPU:0, one launch (start us, length us, event | category | flops | bytes accessed | tf_op | source)
XLA Modules:
  0.0 221.8 jit_solution(9031473623313810624)
XLA Ops:
  0.0 0.8 select_reduce_fusion
  0.9 0.2 add.42
  1.1 0.1 add.43
  1.2 1.4 fusion.9.live_ref
  2.6 11.5 %shard_map.118 = bf16[64,8,4096]{2,1,0:T(8,128)(2,1)} custom-call(bf16[8,4096]{1,0:T(8,128)(2,1)} %q_ref.1, bf16[5888,512]{1,0:T(8,128)(2,1)} %bitcast.21, bf16[5888,512]{1,0:T(8,128)(2,1)} %bitcast.22, s32[8,5888]{1,0:T(8,128)} %fusion.9.live_ref, bf16[8,512]{1,0:T(8,128)(2,1)} %nk_ref.1, bf16[8,512]{1,0:T(8,128)(2,1)} %nv_ref.1), custom_call_target="tpu_custom_call" | custom-call | tf_op jit(solution)/shard_map/pallas_call | solution.py:65
  14.2 11.9 %all-to-all-start = ((bf16[64,8,4096]{2,1,0:T(8,128)(2,1)}), bf16[64,8,4096]{2,1,0:T(8,128)(2,1)}, u32[]{:S(2)}, u32[]{:S(2)}) async-start(bf16[64,8,4096]{2,1,0:T(8,128)(2,1)} %shard_map.118), calls=%async_computation | async-start | bytes 8388608 | tf_op jit(solution)/shard_map/all_to_all | solution.py:122
  26.1 0.1 constant_dynamic-slice_fusion.1
  26.3 1.9 collective-permute-done
  28.2 50.1 %all-to-all-done = bf16[64,8,4096]{2,1,0:T(8,128)(2,1)} async-done(((bf16[64,8,4096]{2,1,0:T(8,128)(2,1)}), bf16[64,8,4096]{2,1,0:T(8,128)(2,1)}, u32[]{:S(2)}, u32[]{:S(2)}) %all-to-all-start) | async-done | bytes 4194336 | tf_op jit(solution)/shard_map/all_to_all | solution.py:122
  78.4 3.7 %fusion = f32[512,128]{0,1:T(8,128)S(1)} fusion(bf16[64,8,4096]{2,1,0:T(8,128)(2,1)} %all-to-all-done, bf16[4096,64]{0,1:T(8,128)(2,1)S(1)} %collective-permute-done, bf16[4096,64]{0,1:T(8,128)(2,1)S(1)} %get-tuple-element.5), kind=kOutput, calls=%fused_computation.1 | convolution fusion | flops 538968064 | bytes 5505024 | tf_op jit(solution)/shard_map/dot_general | solution.py:125
  82.2 1.3 collective-permute-done.1
  83.6 0.5 broadcast_in_dim.7
  84.1 66.3 %all_to_all.15 = bf16[64,64,512]{2,1,0:T(8,128)(2,1)S(1)} all-to-all(bf16[64,64,512]{2,1,0:T(8,128)(2,1)S(1)} %broadcast_in_dim.7), channel_id=1, replica_groups=mesh['head'=2,'req'=64] {'req'}, dimensions={0} | all-to-all | bytes 8388608 | tf_op jit(solution)/shard_map/all_to_all | solution.py:91
  150.4 2.0 fusion.15
  152.5 2.1 fusion.16
  154.5 0.1 pad_maximum_fusion
  154.7 0.3 collective-permute-start.2
  154.9 3.8 %collective-permute-done.2 = f32[512,896]{0,1:T(8,128)S(1)} collective-permute-done((f32[512,896]{0,1:T(8,128)S(1)}, f32[512,896]{0,1:T(8,128)S(1)}, u32[]{:S(2)}, u32[]{:S(2)}) %collective-permute-start.2) | collective-permute-done | bytes 1835040 | tf_op jit(solution)/shard_map/ppermute | solution.py:137
  158.7 0.4 fusion.14
  159.1 2.5 %fusion.6 = f32[512,4096]{0,1:S(1)} fusion(bf16[448,4096]{1,0:T(8,128)(2,1)S(1)} %copy-done.4, f32[512,896]{0,1:T(8,128)S(1)} %fusion.14), kind=kOutput, calls=%fused_computation.10 | convolution fusion | flops 1880424448 | bytes 13893632
  161.7 0.6 convert_bitcast_fusion
  162.3 58.2 %all_to_all.16 = bf16[64,512,64]{1,2,0:T(8,128)(2,1)S(1)} all-to-all(bf16[64,512,64]{1,2,0:T(8,128)(2,1)S(1)} %convert_bitcast_fusion), channel_id=1, replica_groups=mesh['head'=2,'req'=64] {'req'}, dimensions={0} | all-to-all | bytes 8388608 | tf_op jit(solution)/shard_map/all_to_all | solution.py:146
  220.5 0.6 convert_reduce_fusion
  221.2 0.6 add_convert_fusion
  (17 shorter events, 0.3 us)
Async XLA Ops:
  14.2 11.9 %copy-start = (bf16[8192,64]{0,1:T(8,128)(2,1)S(1)}, bf16[8192,64]{0,1:T(8,128)(2,1)}, u32[]{:S(2)}) copy-start(bf16[8192,64]{0,1:T(8,128)(2,1)} %param.20) | copy-start | bytes 3145732
  14.2 64.2 %all-to-all-start = ((bf16[64,8,4096]{2,1,0:T(8,128)(2,1)}), bf16[64,8,4096]{2,1,0:T(8,128)(2,1)}, u32[]{:S(2)}, u32[]{:S(2)}) async-start(bf16[64,8,4096]{2,1,0:T(8,128)(2,1)} %shard_map.118), calls=%async_computation | async-start | bytes 8388608 | tf_op jit(solution)/shard_map/all_to_all | solution.py:122
  26.2 57.3 %copy-start.1 = (bf16[512,64]{0,1:T(8,128)(2,1)S(1)}, bf16[512,64]{0,1:T(8,128)(2,1)}, u32[]{:S(2)}) copy-start(bf16[512,64]{0,1:T(8,128)(2,1)} %param.19) | copy-start | bytes 196612
  26.3 2.0 collective-permute-start
  82.1 1.4 collective-permute-start.1
  84.1 66.3 %copy-start.2 = (bf16[4096,448]{0,1:T(8,128)(2,1)S(1)}, bf16[4096,448]{0,1:T(8,128)(2,1)}, u32[]{:S(2)}) copy-start(bf16[4096,448]{0,1:T(8,128)(2,1)} %param.21) | copy-start | bytes 11010052
  150.4 2.1 copy-start.3
  154.7 4.5 %copy-start.4 = (bf16[448,4096]{1,0:T(8,128)(2,1)S(1)}, bf16[448,4096]{1,0:T(8,128)(2,1)}, u32[]{:S(2)}) copy-start(bf16[448,4096]{1,0:T(8,128)(2,1)} %param.23) | copy-start | bytes 11010052
  154.7 4.0 %collective-permute-start.2 = (f32[512,896]{0,1:T(8,128)S(1)}, f32[512,896]{0,1:T(8,128)S(1)}, u32[]{:S(2)}, u32[]{:S(2)}) collective-permute-start(f32[512,896]{0,1:T(8,128)S(1)} %pad_maximum_fusion), channel_id=1, source_target_pairs={{0,64},{64,0},{1,65},{65,1},{2,66},{66,2},{3,67},{67,3},{4,68},{68... | collective-permute-start | bytes 5505032 | tf_op jit(solution)/shard_map/ppermute | solution.py:137

commit v11 on v10

--- a/solution.py
+++ b/solution.py
@@ -122,11 +122,8 @@
     features = lax.all_to_all(attention_copies, "req", 0, 0, tiled=True).reshape(
         -1, attention_copies.shape[2]
     )
-    both = jnp.dot(
-        features,
-        jnp.concatenate([own_rows, lent_rows], axis=1),
-        preferred_element_type=jnp.float32,
-    )
+    both_rows = lax.optimization_barrier(jnp.concatenate([own_rows, lent_rows], axis=1))
+    both = jnp.dot(features, both_rows, preferred_element_type=jnp.float32)
     attn_update = both[:, :cols] + lax.ppermute(both[:, cols:], "head", swap)
     mixed_rows = (residual.astype(jnp.float32) + attn_update).astype(jnp.bfloat16)
     shard_piece = gather_rows(mixed_rows.T, n_req).reshape(n_req, *mixed_rows.T.shape)

time: 222 us -> 222 us (level)
  no operation moved by 1% of the time
where the time goes in v11:
time: 222 us
  blocking collectives  124 us (56%)
  waiting for transfers between devices  57.1 us (26%)
  starting transfers between devices  12.4 us (6%)
  Pallas kernels  11.5 us (5%)
  matrix products  10.3 us (5%)
  other arithmetic  4.81 us (2%)
    all_to_all x1, blocking collectives, gather_rows(): gathered = lax.all_to_all(copies, 'req', 0, 0, tiled=True)  66.3 us
    all_to_all x1, blocking collectives, body(): gathered = lax.all_to_all(pieces, 'req', 0, 0, tiled=True)  58.2 us
    all_to_all x1, waiting for transfers between devices, body(): lax.all_to_all(attention_copies, 'req', 0, 0, tiled=True)  50.1 us
    all_to_all x1, starting transfers between devices, body(): lax.all_to_all(attention_copies, 'req', 0, 0, tiled=True)  11.9 us
    pallas_call x1, Pallas kernels, attend_pool(): pl.pallas_call(softmax_kernel, grid=(groups,), out_shape=jax.ShapeDtypeSt...  11.5 us
  transfers between devices with their start and end apart: 4, of which 4 were waited for; matrix products, arithmetic and copies ran while one was open for 0% of the time, Pallas kernels for 0%

profile of v11, /device:TPU:0, one launch (start us, length us, event | category | flops | bytes accessed | tf_op | source)
XLA Modules:
  0.0 221.8 jit_solution(16631885037671217568)
XLA Ops:
  0.0 0.8 select_reduce_fusion
  0.9 0.2 add.42
  1.1 0.1 add.43
  1.2 1.4 fusion.6.live_ref
  2.6 11.5 %shard_map.118 = bf16[64,8,4096]{2,1,0:T(8,128)(2,1)} custom-call(bf16[8,4096]{1,0:T(8,128)(2,1)} %q_ref.1, bf16[5888,512]{1,0:T(8,128)(2,1)} %bitcast.22, bf16[5888,512]{1,0:T(8,128)(2,1)} %bitcast.23, s32[8,5888]{1,0:T(8,128)} %fusion.6.live_ref, bf16[8,512]{1,0:T(8,128)(2,1)} %nk_ref.1, bf16[8,512]{1,0:T(8,128)(2,1)} %nv_ref.1), custom_call_target="tpu_custom_call" | custom-call | tf_op jit(solution)/shard_map/pallas_call | solution.py:65
  14.2 11.9 %all-to-all-start = ((bf16[64,8,4096]{2,1,0:T(8,128)(2,1)}), bf16[64,8,4096]{2,1,0:T(8,128)(2,1)}, u32[]{:S(2)}, u32[]{:S(2)}) async-start(bf16[64,8,4096]{2,1,0:T(8,128)(2,1)} %shard_map.118), calls=%async_computation | async-start | bytes 8388608 | tf_op jit(solution)/shard_map/all_to_all | solution.py:122
  26.2 0.1 collective-permute-start
  26.3 1.9 collective-permute-done
  28.3 50.1 %all-to-all-done = bf16[64,8,4096]{2,1,0:T(8,128)(2,1)} async-done(((bf16[64,8,4096]{2,1,0:T(8,128)(2,1)}), bf16[64,8,4096]{2,1,0:T(8,128)(2,1)}, u32[]{:S(2)}, u32[]{:S(2)}) %all-to-all-start) | async-done | bytes 4194336 | tf_op jit(solution)/shard_map/all_to_all | solution.py:122
  78.4 3.7 %fusion = f32[512,128]{0,1:T(8,128)S(1)} fusion(bf16[4096,128]{0,1:T(8,128)(2,1)S(1)} %pad_maximum_fusion.1, bf16[64,8,4096]{2,1,0:T(8,128)(2,1)} %all-to-all-done), kind=kOutput, calls=%fused_computation.1 | convolution fusion | flops 536870912 | bytes 5505024 | tf_op jit(solution)/shard_map/dot_general | solution.py:126
  82.2 1.3 collective-permute-done.1
  83.6 0.5 broadcast_in_dim.7
  84.1 66.3 %all_to_all.15 = bf16[64,64,512]{2,1,0:T(8,128)(2,1)S(1)} all-to-all(bf16[64,64,512]{2,1,0:T(8,128)(2,1)S(1)} %broadcast_in_dim.7), channel_id=1, replica_groups=mesh['head'=2,'req'=64] {'req'}, dimensions={0} | all-to-all | bytes 8388608 | tf_op jit(solution)/shard_map/all_to_all | solution.py:91
  150.4 2.0 fusion.11
  152.5 2.1 fusion.12
  154.5 0.1 pad_maximum_fusion
  154.7 0.3 collective-permute-start.2
  154.9 3.8 %collective-permute-done.2 = f32[512,896]{0,1:T(8,128)S(1)} collective-permute-done((f32[512,896]{0,1:T(8,128)S(1)}, f32[512,896]{0,1:T(8,128)S(1)}, u32[]{:S(2)}, u32[]{:S(2)}) %collective-permute-start.2) | collective-permute-done | bytes 1835040 | tf_op jit(solution)/shard_map/ppermute | solution.py:134
  158.7 0.4 fusion.10
  159.1 2.5 %fusion.3 = f32[512,4096]{0,1:S(1)} fusion(bf16[448,4096]{1,0:T(8,128)(2,1)S(1)} %copy-done.4, f32[512,896]{0,1:T(8,128)S(1)} %fusion.10), kind=kOutput, calls=%fused_computation.8 | convolution fusion | flops 1880424448 | bytes 13893632
  161.7 0.6 convert_bitcast_fusion
  162.3 58.2 %all_to_all.16 = bf16[64,512,64]{1,2,0:T(8,128)(2,1)S(1)} all-to-all(bf16[64,512,64]{1,2,0:T(8,128)(2,1)S(1)} %convert_bitcast_fusion), channel_id=1, replica_groups=mesh['head'=2,'req'=64] {'req'}, dimensions={0} | all-to-all | bytes 8388608 | tf_op jit(solution)/shard_map/all_to_all | solution.py:143
  220.5 0.6 convert_reduce_fusion
  221.2 0.6 add_convert_fusion
  (18 shorter events, 0.4 us)
Async XLA Ops:
  14.2 11.9 %copy-start = (bf16[8192,64]{0,1:T(8,128)(2,1)S(1)}, bf16[8192,64]{0,1:T(8,128)(2,1)}, u32[]{:S(2)}) copy-start(bf16[8192,64]{0,1:T(8,128)(2,1)} %param.20) | copy-start | bytes 3145732
  14.2 64.2 %all-to-all-start = ((bf16[64,8,4096]{2,1,0:T(8,128)(2,1)}), bf16[64,8,4096]{2,1,0:T(8,128)(2,1)}, u32[]{:S(2)}, u32[]{:S(2)}) async-start(bf16[64,8,4096]{2,1,0:T(8,128)(2,1)} %shard_map.118), calls=%async_computation | async-start | bytes 8388608 | tf_op jit(solution)/shard_map/all_to_all | solution.py:122
  26.2 2.0 collective-permute-start
  28.2 55.3 %copy-start.1 = (bf16[512,64]{0,1:T(8,128)(2,1)S(1)}, bf16[512,64]{0,1:T(8,128)(2,1)}, u32[]{:S(2)}) copy-start(bf16[512,64]{0,1:T(8,128)(2,1)} %param.19) | copy-start | bytes 196612
  82.1 1.4 collective-permute-start.1
  84.1 66.3 %copy-start.2 = (bf16[4096,448]{0,1:T(8,128)(2,1)S(1)}, bf16[4096,448]{0,1:T(8,128)(2,1)}, u32[]{:S(2)}) copy-start(bf16[4096,448]{0,1:T(8,128)(2,1)} %param.21) | copy-start | bytes 11010052
  150.4 2.1 copy-start.3
  154.7 4.5 %copy-start.4 = (bf16[448,4096]{1,0:T(8,128)(2,1)S(1)}, bf16[448,4096]{1,0:T(8,128)(2,1)}, u32[]{:S(2)}) copy-start(bf16[448,4096]{1,0:T(8,128)(2,1)} %param.23) | copy-start | bytes 11010052
  154.7 4.0 %collective-permute-start.2 = (f32[512,896]{0,1:T(8,128)S(1)}, f32[512,896]{0,1:T(8,128)S(1)}, u32[]{:S(2)}, u32[]{:S(2)}) collective-permute-start(f32[512,896]{0,1:T(8,128)S(1)} %pad_maximum_fusion), channel_id=1, source_target_pairs={{0,64},{64,0},{1,65},{65,1},{2,66},{66,2},{3,67},{67,3},{4,68},{68... | collective-permute-start | bytes 5505032 | tf_op jit(solution)/shard_map/ppermute | solution.py:134

commit v12 on v11

--- a/solution.py
+++ b/solution.py
@@ -122,9 +122,9 @@
     features = lax.all_to_all(attention_copies, "req", 0, 0, tiled=True).reshape(
         -1, attention_copies.shape[2]
     )
-    both_rows = lax.optimization_barrier(jnp.concatenate([own_rows, lent_rows], axis=1))
-    both = jnp.dot(features, both_rows, preferred_element_type=jnp.float32)
-    attn_update = both[:, :cols] + lax.ppermute(both[:, cols:], "head", swap)
+    for_partner = jnp.dot(features, lent_rows, preferred_element_type=jnp.float32)
+    from_partner = lax.ppermute(for_partner, "head", swap)
+    attn_update = jnp.dot(features, own_rows, preferred_element_type=jnp.float32) + from_partner
     mixed_rows = (residual.astype(jnp.float32) + attn_update).astype(jnp.bfloat16)
     shard_piece = gather_rows(mixed_rows.T, n_req).reshape(n_req, *mixed_rows.T.shape)
     shard_piece = shard_piece.transpose(2, 0, 1).reshape(mixed_rows.shape[0], -1)

time: 222 us -> 225 us (1.014)
  matrix products: 10.3 us -> 13.8 us
    dot_general x1 -> x2, matrix products: 3.71 us -> 7.16 us  [the longest x1 3.59 us: body(): jnp.dot(features, own_rows, preferred_element_type=jnp.float32)]
  transfers between devices with their start and end apart: 4 -> 4, of which waited for: 4 -> 3; matrix products, arithmetic and copies ran while one was open for 0% -> 2% of each run, Pallas kernels for 0% -> 0%
where the time goes in v12:
time: 225 us; the launch traced here: 224 us
  blocking collectives  125 us (56%)
  waiting for transfers between devices  55.8 us (25%)
  matrix products  13.8 us (6%)
  starting transfers between devices  12.2 us (5%)
  Pallas kernels  11.5 us (5%)
  other arithmetic  4.83 us (2%)
    all_to_all x1, blocking collectives, gather_rows(): gathered = lax.all_to_all(copies, 'req', 0, 0, tiled=True)  66.5 us
    all_to_all x1, blocking collectives, body(): gathered = lax.all_to_all(pieces, 'req', 0, 0, tiled=True)  58.3 us
    all_to_all x1, waiting for transfers between devices, body(): lax.all_to_all(attention_copies, 'req', 0, 0, tiled=True)  50.2 us
    all_to_all x1, starting transfers between devices, body(): lax.all_to_all(attention_copies, 'req', 0, 0, tiled=True)  11.8 us
    pallas_call x1, Pallas kernels, attend_pool(): pl.pallas_call(softmax_kernel, grid=(groups,), out_shape=jax.ShapeDtypeSt...  11.5 us
  transfers between devices with their start and end apart: 4, of which 3 were waited for; matrix products, arithmetic and copies ran while one was open for 2% of the time, Pallas kernels for 0%

profile of v12, /device:TPU:0, one launch (start us, length us, event | category | flops | bytes accessed | tf_op | source)
XLA Modules:
  0.0 224.2 jit_solution(11928788488406809731)
XLA Ops:
  0.0 0.9 select_reduce_fusion
  1.0 0.2 add.42
  1.2 0.1 add.43
  1.3 1.4 fusion.9.live_ref
  2.7 11.5 %shard_map.118 = bf16[64,8,4096]{2,1,0:T(8,128)(2,1)} custom-call(bf16[8,4096]{1,0:T(8,128)(2,1)} %q_ref.1, bf16[5888,512]{1,0:T(8,128)(2,1)} %bitcast.24, bf16[5888,512]{1,0:T(8,128)(2,1)} %bitcast.25, s32[8,5888]{1,0:T(8,128)} %fusion.9.live_ref, bf16[8,512]{1,0:T(8,128)(2,1)} %nk_ref.1, bf16[8,512]{1,0:T(8,128)(2,1)} %nv_ref.1), custom_call_target="tpu_custom_call" | custom-call | tf_op jit(solution)/shard_map/pallas_call | solution.py:65
  14.3 11.8 %all-to-all-start = ((bf16[64,8,4096]{2,1,0:T(8,128)(2,1)}), bf16[64,8,4096]{2,1,0:T(8,128)(2,1)}, u32[]{:S(2)}, u32[]{:S(2)}) async-start(bf16[64,8,4096]{2,1,0:T(8,128)(2,1)} %shard_map.118), calls=%async_computation | async-start | bytes 8388608 | tf_op jit(solution)/shard_map/all_to_all | solution.py:122
  26.1 0.1 collective-permute-start
  26.3 1.9 collective-permute-done
  28.1 50.2 %all-to-all-done = bf16[64,8,4096]{2,1,0:T(8,128)(2,1)} async-done(((bf16[64,8,4096]{2,1,0:T(8,128)(2,1)}), bf16[64,8,4096]{2,1,0:T(8,128)(2,1)}, u32[]{:S(2)}, u32[]{:S(2)}) %all-to-all-start) | async-done | bytes 4194336 | tf_op jit(solution)/shard_map/all_to_all | solution.py:122
  78.3 3.6 %fusion = f32[512,64]{0,1:T(8,128)S(1)} fusion(bf16[4096,64]{0,1:T(8,128)(2,1)S(1)} %collective-permute-done, bf16[64,8,4096]{2,1,0:T(8,128)(2,1)} %all-to-all-done), kind=kOutput, calls=%fused_computation.1 | convolution fusion | flops 268435456 | bytes 4849664 | tf_op jit(solution)/shard_map/dot_general | solution.py:125
  82.0 3.6 %fusion.2 = f32[512,64]{0,1:T(8,128)S(1)} fusion(bf16[64,8,4096]{2,1,0:T(8,128)(2,1)} %all-to-all-done, bf16[8192,64]{0,1:T(8,128)(2,1)S(1)} %copy-done, s32[]{:T(128)S(6)} %select_n.11), kind=kOutput, calls=%fused_computation.3 | convolution fusion | flops 268435456 | bytes 4849668 | tf_op jit(solution)/shard_map/dot_general | solution.py:127
  85.6 0.5 broadcast_in_dim.7
  86.1 66.5 %all_to_all.15 = bf16[64,64,512]{2,1,0:T(8,128)(2,1)S(1)} all-to-all(bf16[64,64,512]{2,1,0:T(8,128)(2,1)S(1)} %broadcast_in_dim.7), channel_id=1, replica_groups=mesh['head'=2,'req'=64] {'req'}, dimensions={0} | all-to-all | bytes 8388608 | tf_op jit(solution)/shard_map/all_to_all | solution.py:91
  152.6 2.0 fusion.13
  154.7 2.0 fusion.14
  156.7 0.1 pad_maximum_fusion
  156.9 0.3 collective-permute-start.2
  157.2 3.8 %collective-permute-done.2 = f32[512,896]{0,1:T(8,128)S(1)} collective-permute-done((f32[512,896]{0,1:T(8,128)S(1)}, f32[512,896]{0,1:T(8,128)S(1)}, u32[]{:S(2)}, u32[]{:S(2)}) %collective-permute-start.2) | collective-permute-done | bytes 1835040 | tf_op jit(solution)/shard_map/ppermute | solution.py:134
  160.9 0.4 fusion.12
  161.4 2.5 %fusion.6 = f32[512,4096]{0,1:S(1)} fusion(bf16[448,4096]{1,0:T(8,128)(2,1)S(1)} %copy-done.5, f32[512,896]{0,1:T(8,128)S(1)} %fusion.12), kind=kOutput, calls=%fused_computation.10 | convolution fusion | flops 1880424448 | bytes 13893632
  163.9 0.6 convert_bitcast_fusion
  164.6 58.3 %all_to_all.16 = bf16[64,512,64]{1,2,0:T(8,128)(2,1)S(1)} all-to-all(bf16[64,512,64]{1,2,0:T(8,128)(2,1)S(1)} %convert_bitcast_fusion), channel_id=1, replica_groups=mesh['head'=2,'req'=64] {'req'}, dimensions={0} | all-to-all | bytes 8388608 | tf_op jit(solution)/shard_map/all_to_all | solution.py:143
  222.9 0.6 convert_reduce_fusion
  223.5 0.6 add_convert_fusion
  (19 shorter events, 0.3 us)
Async XLA Ops:
  0.0 26.1 %copy-start = (bf16[8192,64]{0,1:T(8,128)(2,1)S(1)}, bf16[8192,64]{0,1:T(8,128)(2,1)}, u32[]{:S(2)}) copy-start(bf16[8192,64]{0,1:T(8,128)(2,1)} %param.20) | copy-start | bytes 3145732
  14.3 64.0 %all-to-all-start = ((bf16[64,8,4096]{2,1,0:T(8,128)(2,1)}), bf16[64,8,4096]{2,1,0:T(8,128)(2,1)}, u32[]{:S(2)}, u32[]{:S(2)}) async-start(bf16[64,8,4096]{2,1,0:T(8,128)(2,1)} %shard_map.118), calls=%async_computation | async-start | bytes 8388608 | tf_op jit(solution)/shard_map/all_to_all | solution.py:122
  26.1 2.0 collective-permute-start
  26.2 59.3 %copy-start.2 = (bf16[512,64]{0,1:T(8,128)(2,1)S(1)}, bf16[512,64]{0,1:T(8,128)(2,1)}, u32[]{:S(2)}) copy-start(bf16[512,64]{0,1:T(8,128)(2,1)} %param.19) | copy-start | bytes 196612
  81.9 3.7 %collective-permute-start.1 = (f32[512,64]{0,1:T(8,128)S(1)}, f32[512,64]{0,1:T(8,128)S(1)}, u32[]{:S(2)}, u32[]{:S(2)}) collective-permute-start(f32[512,64]{0,1:T(8,128)S(1)} %fusion), channel_id=1, source_target_pairs={{0,64},{64,0},{1,65},{65,1},{2,66},{66,2},{3,67},{67,3},{4,68},{68... | collective-permute-start | bytes 393224 | tf_op jit(solution)/shard_map/ppermute | solution.py:126
  86.1 66.5 %copy-start.3 = (bf16[4096,448]{0,1:T(8,128)(2,1)S(1)}, bf16[4096,448]{0,1:T(8,128)(2,1)}, u32[]{:S(2)}) copy-start(bf16[4096,448]{0,1:T(8,128)(2,1)} %param.21) | copy-start | bytes 11010052
  152.6 2.1 copy-start.4
  156.7 4.6 %copy-start.5 = (bf16[448,4096]{1,0:T(8,128)(2,1)S(1)}, bf16[448,4096]{1,0:T(8,128)(2,1)}, u32[]{:S(2)}) copy-start(bf16[448,4096]{1,0:T(8,128)(2,1)} %param.23) | copy-start | bytes 11010052
  156.9 4.0 %collective-permute-start.2 = (f32[512,896]{0,1:T(8,128)S(1)}, f32[512,896]{0,1:T(8,128)S(1)}, u32[]{:S(2)}, u32[]{:S(2)}) collective-permute-start(f32[512,896]{0,1:T(8,128)S(1)} %pad_maximum_fusion), channel_id=1, source_target_pairs={{0,64},{64,0},{1,65},{65,1},{2,66},{66,2},{3,67},{67,3},{4,68},{68... | collective-permute-start | bytes 5505032 | tf_op jit(solution)/shard_map/ppermute | solution.py:134
  164.5 59.6 %copy-start.1 = (bf16[8192,64]{0,1:T(8,128)(2,1)S(1)}, bf16[8192,64]{0,1:T(8,128)(2,1)}, u32[]{:S(2)}) copy-start(bf16[8192,64]{0,1:T(8,128)(2,1)} %param.20) | copy-start | bytes 3145732

commit v13 on v10

--- a/solution.py
+++ b/solution.py
@@ -129,8 +129,8 @@
     )
     attn_update = both[:, :cols] + lax.ppermute(both[:, cols:], "head", swap)
     mixed_rows = (residual.astype(jnp.float32) + attn_update).astype(jnp.bfloat16)
-    shard_piece = gather_rows(mixed_rows.T, n_req).reshape(n_req, *mixed_rows.T.shape)
-    shard_piece = shard_piece.transpose(2, 0, 1).reshape(mixed_rows.shape[0], -1)
+    shard_piece = gather_rows(mixed_rows, n_req).reshape(n_req, *mixed_rows.shape)
+    shard_piece = shard_piece.transpose(1, 0, 2).reshape(mixed_rows.shape[0], -1)
     gate_acts = jnp.dot(shard_piece, gate_weight, preferred_element_type=jnp.float32)
     up_acts = jnp.dot(shard_piece, up_weight, preferred_element_type=jnp.float32)
     acts = jnp.concatenate([gate_acts, up_acts], axis=1)

time: 222 us -> 222 us (level)
  no operation moved by 1% of the time
where the time goes in v13:
time: 222 us
  blocking collectives  124 us (56%)
  waiting for transfers between devices  57.1 us (26%)
  starting transfers between devices  12.4 us (6%)
  Pallas kernels  11.5 us (5%)
  matrix products  10.3 us (5%)
  other arithmetic  4.74 us (2%)
    all_to_all x1, blocking collectives, gather_rows(): gathered = lax.all_to_all(copies, 'req', 0, 0, tiled=True)  66.3 us
    all_to_all x1, blocking collectives, body(): gathered = lax.all_to_all(pieces, 'req', 0, 0, tiled=True)  58.2 us
    all_to_all x1, waiting for transfers between devices, body(): lax.all_to_all(attention_copies, 'req', 0, 0, tiled=True)  50.1 us
    all_to_all x1, starting transfers between devices, body(): lax.all_to_all(attention_copies, 'req', 0, 0, tiled=True)  11.9 us
    pallas_call x1, Pallas kernels, attend_pool(): pl.pallas_call(softmax_kernel, grid=(groups,), out_shape=jax.ShapeDtypeSt...  11.5 us
  transfers between devices with their start and end apart: 4, of which 4 were waited for; matrix products, arithmetic and copies ran while one was open for 0% of the time, Pallas kernels for 0%

profile of v13, /device:TPU:0, one launch (start us, length us, event | category | flops | bytes accessed | tf_op | source)
XLA Modules:
  0.0 221.8 jit_solution(10917949311690768107)
XLA Ops:
  0.0 0.8 select_reduce_fusion
  0.9 0.2 add.42
  1.1 0.1 add.43
  1.2 1.4 fusion.9.live_ref
  2.6 11.5 %shard_map.118 = bf16[64,8,4096]{2,1,0:T(8,128)(2,1)} custom-call(bf16[8,4096]{1,0:T(8,128)(2,1)} %q_ref.1, bf16[5888,512]{1,0:T(8,128)(2,1)} %bitcast.20, bf16[5888,512]{1,0:T(8,128)(2,1)} %bitcast.21, s32[8,5888]{1,0:T(8,128)} %fusion.9.live_ref, bf16[8,512]{1,0:T(8,128)(2,1)} %nk_ref.1, bf16[8,512]{1,0:T(8,128)(2,1)} %nv_ref.1), custom_call_target="tpu_custom_call" | custom-call | tf_op jit(solution)/shard_map/pallas_call | solution.py:65
  14.2 11.9 %all-to-all-start = ((bf16[64,8,4096]{2,1,0:T(8,128)(2,1)}), bf16[64,8,4096]{2,1,0:T(8,128)(2,1)}, u32[]{:S(2)}, u32[]{:S(2)}) async-start(bf16[64,8,4096]{2,1,0:T(8,128)(2,1)} %shard_map.118), calls=%async_computation | async-start | bytes 8388608 | tf_op jit(solution)/shard_map/all_to_all | solution.py:122
  26.1 0.1 constant_dynamic-slice_fusion.1
  26.3 1.9 collective-permute-done
  28.2 50.1 %all-to-all-done = bf16[64,8,4096]{2,1,0:T(8,128)(2,1)} async-done(((bf16[64,8,4096]{2,1,0:T(8,128)(2,1)}), bf16[64,8,4096]{2,1,0:T(8,128)(2,1)}, u32[]{:S(2)}, u32[]{:S(2)}) %all-to-all-start) | async-done | bytes 4194336 | tf_op jit(solution)/shard_map/all_to_all | solution.py:122
  78.4 3.7 %fusion = f32[512,128]{0,1:T(8,128)S(1)} fusion(bf16[64,8,4096]{2,1,0:T(8,128)(2,1)} %all-to-all-done, bf16[4096,64]{0,1:T(8,128)(2,1)S(1)} %collective-permute-done, bf16[4096,64]{0,1:T(8,128)(2,1)S(1)} %get-tuple-element.5), kind=kOutput, calls=%fused_computation.1 | convolution fusion | flops 538968064 | bytes 5505024 | tf_op jit(solution)/shard_map/dot_general | solution.py:125
  82.2 1.3 collective-permute-done.1
  83.6 0.5 broadcast_in_dim.7
  84.1 66.3 %all_to_all.15 = bf16[64,512,64]{1,2,0:T(8,128)(2,1)S(1)} all-to-all(bf16[64,512,64]{1,2,0:T(8,128)(2,1)S(1)} %broadcast_in_dim.7), channel_id=1, replica_groups=mesh['head'=2,'req'=64] {'req'}, dimensions={0} | all-to-all | bytes 8388608 | tf_op jit(solution)/shard_map/all_to_all | solution.py:91
  150.4 2.0 fusion.15
  152.5 2.1 fusion.16
  154.5 0.1 pad_maximum_fusion
  154.7 0.3 collective-permute-start.2
  154.9 3.8 %collective-permute-done.2 = f32[512,896]{0,1:T(8,128)S(1)} collective-permute-done((f32[512,896]{0,1:T(8,128)S(1)}, f32[512,896]{0,1:T(8,128)S(1)}, u32[]{:S(2)}, u32[]{:S(2)}) %collective-permute-start.2) | collective-permute-done | bytes 1835040 | tf_op jit(solution)/shard_map/ppermute | solution.py:137
  158.7 0.4 fusion.14
  159.1 2.5 %fusion.6 = f32[512,4096]{0,1:S(1)} fusion(bf16[448,4096]{1,0:T(8,128)(2,1)S(1)} %copy-done.4, f32[512,896]{0,1:T(8,128)S(1)} %fusion.14), kind=kOutput, calls=%fused_computation.10 | convolution fusion | flops 1880424448 | bytes 13893632
  161.7 0.6 convert_bitcast_fusion
  162.3 58.2 %all_to_all.16 = bf16[64,512,64]{1,2,0:T(8,128)(2,1)S(1)} all-to-all(bf16[64,512,64]{1,2,0:T(8,128)(2,1)S(1)} %convert_bitcast_fusion), channel_id=1, replica_groups=mesh['head'=2,'req'=64] {'req'}, dimensions={0} | all-to-all | bytes 8388608 | tf_op jit(solution)/shard_map/all_to_all | solution.py:146
  220.5 0.6 convert_reduce_fusion
  221.2 0.6 add_convert_fusion
  (17 shorter events, 0.3 us)
Async XLA Ops:
  14.2 11.9 %copy-start = (bf16[8192,64]{0,1:T(8,128)(2,1)S(1)}, bf16[8192,64]{0,1:T(8,128)(2,1)}, u32[]{:S(2)}) copy-start(bf16[8192,64]{0,1:T(8,128)(2,1)} %param.20) | copy-start | bytes 3145732
  14.2 64.2 %all-to-all-start = ((bf16[64,8,4096]{2,1,0:T(8,128)(2,1)}), bf16[64,8,4096]{2,1,0:T(8,128)(2,1)}, u32[]{:S(2)}, u32[]{:S(2)}) async-start(bf16[64,8,4096]{2,1,0:T(8,128)(2,1)} %shard_map.118), calls=%async_computation | async-start | bytes 8388608 | tf_op jit(solution)/shard_map/all_to_all | solution.py:122
  26.2 57.3 %copy-start.1 = (bf16[512,64]{0,1:T(8,128)(2,1)S(1)}, bf16[512,64]{0,1:T(8,128)(2,1)}, u32[]{:S(2)}) copy-start(bf16[512,64]{0,1:T(8,128)(2,1)} %param.19) | copy-start | bytes 196612
  26.3 2.0 collective-permute-start
  82.1 1.4 collective-permute-start.1
  84.1 66.3 %copy-start.2 = (bf16[4096,448]{0,1:T(8,128)(2,1)S(1)}, bf16[4096,448]{0,1:T(8,128)(2,1)}, u32[]{:S(2)}) copy-start(bf16[4096,448]{0,1:T(8,128)(2,1)} %param.21) | copy-start | bytes 11010052
  150.4 2.1 copy-start.3
  154.7 4.5 %copy-start.4 = (bf16[448,4096]{1,0:T(8,128)(2,1)S(1)}, bf16[448,4096]{1,0:T(8,128)(2,1)}, u32[]{:S(2)}) copy-start(bf16[448,4096]{1,0:T(8,128)(2,1)} %param.23) | copy-start | bytes 11010052
  154.7 4.0 %collective-permute-start.2 = (f32[512,896]{0,1:T(8,128)S(1)}, f32[512,896]{0,1:T(8,128)S(1)}, u32[]{:S(2)}, u32[]{:S(2)}) collective-permute-start(f32[512,896]{0,1:T(8,128)S(1)} %pad_maximum_fusion), channel_id=1, source_target_pairs={{0,64},{64,0},{1,65},{65,1},{2,66},{66,2},{3,67},{67,3},{4,68},{68... | collective-permute-start | bytes 5505032 | tf_op jit(solution)/shard_map/ppermute | solution.py:137
